TPU v7x, 256 devices: a whole 4x4x8 slice. The times are simulated.
256 devices in a mesh: seq: 128 (over z, y, x_lo, core), dp: 2 (over x_hi).
Axes of the slice: x: 4 (x_hi: 2, x_lo: 2; x = x_hi * 2 + x_lo), y: 4, z: 8, core: 2. Of those that a mesh axis runs over, the one named last changes fastest.
Arguments:
- frames: bfloat16 [2, 16384, 1024], P('dp', 'seq'), may hold values from -36 to 36
- kernel: bfloat16 [31, 1024], replicated, may hold values from -1 to 1
- norm_gain: float32 [1024], replicated, may hold values from 0.5 to 1.5
- router: bfloat16 [1024, 32], replicated, may hold values from -0.1875 to 0.1875
- experts: int32 [2, 16384, 2], P('dp', 'seq'), may hold values from 0 to 31, all different within a row; in each aligned block of 128 rows (0 to 127, 128 to 255, ..., all dimensions but the last counted through in order) at most 16 rows name the same one
- w_in: bfloat16 [128, 1024, 512], P('seq'), may hold values from -0.1875 to 0.1875
- w_out: bfloat16 [128, 512, 1024], P('seq'), may hold values from -0.125 to 0.125
- cotangent: bfloat16 [2, 16384, 1024], P('dp', 'seq'), may hold values from -8 to 8
Outputs:
- mixed: bfloat16 [2, 16384, 1024], P('dp', 'seq')
- grad_frames: bfloat16 [2, 16384, 1024], P('dp', 'seq')
- grad_kernel: float32 [31, 1024], replicated
- grad_gain: float32 [1024], replicated
- grad_router: float32 [1024, 32], replicated
- grad_w_in: float32 [128, 1024, 512], P('seq')
- grad_w_out: float32 [128, 512, 1024], P('seq')
Inputs may be any that keep to these rules, and one draw needn't show every extreme that they name: Each frame names 2 different experts; in each aligned block of 128 frames no expert is named more than 16 times, a bound that some block reaches.
All inputs are finite; a program needn't handle non-finite values.
Results may differ from a plain program's by a relative error of at most 0.0075.
Values may be sent and summed in bfloat16 or wider, within the bound.
No kernel may reach another device: no remote copies, remote signals or barrier semaphores. Data moves between devices by JAX's collectives and lax.ppermute only.
A program may use at most 128 MiB of HBM per device.

v0:
```python
import jax
import jax.numpy as jnp
from jax import lax
from jax.sharding import PartitionSpec as P

eps = 1e-06


def padded_2(shard, sides, width):
    for axis, dim in sides:
        size, length = (lax.axis_size(axis), shard.shape[dim])
        up = [(i, (i + 1) % size) for i in range(size - 1)]
        down = [(j, i) for i, j in up]
        last = lax.slice_in_dim(shard, length - width, length, axis=dim)
        initial = lax.slice_in_dim(shard, 0, width, axis=dim)
        before = lax.ppermute(last, axis, up)
        after = lax.ppermute(initial, axis, down)
        shard = jnp.concatenate([before, shard, after], axis=dim)
    return shard


def conv_forward(padded, kernel, row_count):
    summed = jnp.zeros((row_count, padded.shape[1]), jnp.float32)
    for offset in range(kernel.shape[0]):
        summed = summed + kernel[offset].astype(jnp.float32) * padded[
            offset : offset + row_count
        ].astype(jnp.float32)
    return summed


def conv_transpose(padded, kernel, row_count):
    length = kernel.shape[0]
    summed = jnp.zeros((row_count, padded.shape[1]), jnp.float32)
    for offset in range(length):
        start = length - 1 - offset
        summed = summed + kernel[offset].astype(jnp.float32) * padded[start : start + row_count]
    return summed


def kernel_terms(padded, upstream, length, row_count):
    return jnp.stack(
        [
            jnp.sum(padded[offset : offset + row_count].astype(jnp.float32) * upstream, axis=0)
            for offset in range(length)
        ]
    )


def normalize(summed, norm_gain):
    square = jnp.mean(summed * summed, axis=-1, keepdims=True)
    return summed * lax.rsqrt(square + eps) * norm_gain


def slot_numbers(expert_ids, expert_count):
    onehot = (expert_ids[:, None] == jnp.arange(expert_count, dtype=jnp.int32)[None, :]).astype(
        jnp.int32
    )
    ranks = jnp.cumsum(onehot, axis=0) - onehot
    return jnp.sum(ranks * onehot, axis=1)


def gate_values(normed_b, router, first_ids, second_ids):
    logits = jnp.dot(normed_b, router, preferred_element_type=jnp.float32)
    columns = jnp.arange(router.shape[1], dtype=jnp.int32)[None, :]
    pick_diff = (first_ids[:, None] == columns).astype(jnp.float32) - (
        second_ids[:, None] == columns
    ).astype(jnp.float32)
    gate_one = jax.nn.sigmoid(jnp.sum(logits * pick_diff, axis=1))
    return (gate_one, 1.0 - gate_one, pick_diff)


def swish_parts(pre_act):
    squash = jax.nn.sigmoid(pre_act)
    return (pre_act * squash, squash * (1.0 + pre_act * (1.0 - squash)))


def gate_backward(upstream, out_one, out_two, gate_one, gate_two, pick_diff, normed_b, router):
    grad_gap = (
        (jnp.sum(upstream * out_one, axis=1) - jnp.sum(upstream * out_two, axis=1))
        * gate_one
        * gate_two
    )
    grad_logits = (grad_gap[:, None] * pick_diff).astype(jnp.bfloat16)
    router_term = jnp.dot(normed_b.T, grad_logits, preferred_element_type=jnp.float32)
    normed_term = jnp.dot(grad_logits, router.T, preferred_element_type=jnp.float32)
    return (router_term, normed_term)


def combine_back(partial_rows):
    return lax.all_to_all(partial_rows, "seq", split_axis=0, concat_axis=0, tiled=True)


def body(frames, kernel, norm_gain, router, experts, w_in, w_out, cotangent):
    inputs_dev = frames[0]
    row_count = inputs_dev.shape[0]
    width = inputs_dev.shape[1]
    length = kernel.shape[0]
    half_width = length // 2
    expert_count = router.shape[1]
    top_count = experts.shape[2]
    capacity = 2 * row_count * top_count // expert_count
    group_size = lax.axis_size("seq") // expert_count
    in_weights = w_in[0]
    out_weights = w_out[0]
    padded = padded_2(inputs_dev, (("seq", 0),), half_width)
    summed = inputs_dev.astype(jnp.float32) + conv_forward(padded, kernel, row_count)
    normed_b = normalize(summed, norm_gain).astype(jnp.bfloat16)
    choice_ids = experts[0]
    gate_one, gate_two, pick_diff = gate_values(
        normed_b, router, choice_ids[:, 0], choice_ids[:, 1]
    )
    flat_ids = choice_ids.reshape(-1)
    slot_index = slot_numbers(flat_ids, expert_count)
    position = flat_ids * capacity + slot_index
    dispatch_table = (
        lax.broadcasted_iota(jnp.int32, (expert_count * capacity, flat_ids.shape[0]), 0)
        == position[None, :]
    ).astype(jnp.bfloat16)

    def pack(values):
        return jnp.dot(dispatch_table, values, preferred_element_type=jnp.float32).astype(
            jnp.bfloat16
        )

    def spread(values):
        return jnp.repeat(pack(values).reshape(expert_count, capacity, width), group_size, axis=0)

    def slice_totals(returned):
        totals = jnp.sum(
            returned.astype(jnp.float32).reshape(expert_count, group_size, capacity, width), axis=1
        )
        return totals.reshape(expert_count * capacity, width)

    def gather_back(totals):
        picked = jnp.take(totals, position, axis=0)
        return picked.reshape(row_count, top_count, width)

    repeated = jnp.repeat(normed_b, top_count, axis=0)
    upstream = cotangent[0].astype(jnp.float32)
    grad_assigned = jnp.stack([gate_one[:, None] * upstream, gate_two[:, None] * upstream], axis=1)
    grad_values = grad_assigned.reshape(row_count * top_count, width).astype(jnp.bfloat16)
    arrived = lax.all_to_all(spread(repeated), "seq", split_axis=0, concat_axis=0, tiled=True)
    flat_rows = arrived.reshape(-1, width)
    pre_act = jnp.dot(flat_rows, in_weights, preferred_element_type=jnp.float32)
    hidden = swish_parts(pre_act)[0].astype(jnp.bfloat16)
    partial_rows = jnp.dot(hidden, out_weights, preferred_element_type=jnp.float32).astype(
        jnp.bfloat16
    )
    results = (combine_back(partial_rows.reshape(arrived.shape)), arrived)
    arrived = results[1]
    assigned = gather_back(slice_totals(results[0]))
    out_one = assigned[:, 0]
    out_two = assigned[:, 1]
    mixed = (summed + gate_one[:, None] * out_one + gate_two[:, None] * out_two).astype(
        jnp.bfloat16
    )
    incoming = lax.all_to_all(spread(grad_values), "seq", split_axis=0, concat_axis=0, tiled=True)
    flat_rows = arrived.reshape(-1, width)
    flat_grads = incoming.reshape(-1, width)
    pre_act = jnp.dot(flat_rows, in_weights, preferred_element_type=jnp.float32)
    hidden_f, slope = swish_parts(pre_act)
    hidden = hidden_f.astype(jnp.bfloat16)
    grad_hidden = jnp.dot(flat_grads, out_weights.T, preferred_element_type=jnp.float32)
    grad_pre = (grad_hidden * slope).astype(jnp.bfloat16)
    out_term = jnp.dot(hidden.T, flat_grads, preferred_element_type=jnp.float32)
    in_term = jnp.dot(flat_rows.T, grad_pre, preferred_element_type=jnp.float32)
    grad_part = jnp.dot(grad_pre, in_weights.T, preferred_element_type=jnp.float32).astype(
        jnp.bfloat16
    )
    grad_totals = slice_totals(
        lax.all_to_all(
            grad_part.reshape(arrived.shape), "seq", split_axis=0, concat_axis=0, tiled=True
        )
    )
    normed_grads = jnp.sum(gather_back(grad_totals), axis=1)
    router_term, normed_term = gate_backward(
        upstream, out_one, out_two, gate_one, gate_two, pick_diff, normed_b, router
    )
    pullback = jax.vjp(normalize, summed, norm_gain)[1]
    summed_grad, gain_term = pullback(normed_grads + normed_term)
    upstream_total = upstream + summed_grad
    padded_grad = padded_2(upstream_total.astype(jnp.bfloat16), (("seq", 0),), half_width).astype(
        upstream_total.dtype
    )
    grad_frames = (upstream_total + conv_transpose(padded_grad, kernel, row_count)).astype(
        jnp.bfloat16
    )
    kernel_term = kernel_terms(padded, upstream_total, length, row_count)
    grad_kernel, grad_gain, grad_router = lax.psum(
        (kernel_term, gain_term, router_term), ("seq", "dp")
    )
    grad_in, grad_out = (
        lax.psum(in_term.astype(jnp.bfloat16), "dp").astype(jnp.float32),
        lax.psum(out_term.astype(jnp.bfloat16), "dp").astype(jnp.float32),
    )
    return (
        mixed[None],
        grad_frames[None],
        grad_kernel,
        grad_gain,
        grad_router,
        grad_in[None],
        grad_out[None],
    )


def solution(mesh):
    return jax.shard_map(
        body,
        mesh=mesh,
        in_specs=(
            P("dp", "seq", None),
            P(),
            P(),
            P(),
            P("dp", "seq", None),
            P("seq", None, None),
            P("seq", None, None),
            P("dp", "seq", None),
        ),
        out_specs=(
            P("dp", "seq", None),
            P("dp", "seq", None),
            P(),
            P(),
            P(),
            P("seq", None, None),
            P("seq", None, None),
        ),
        check_vma=False,
    )
```

profile of v0, /device:TPU:1, one launch (start us, length us, event | category | flops | bytes accessed | tf_op | source)
XLA Modules:
  0.0 801.1 jit_solution(16135319086898299897)
XLA Ops:
  8.0 0.9 slice_bitcast_fusion.1
  8.9 4.5 collective-permute-start
  13.4 1.9 collective-permute-start.1
  15.3 0.8 copy.15
  16.4 1.0 slice_convert_fusion.29
  17.5 1.2 slice_convert_fusion.30
  18.9 0.6 reduce-window.6
  19.8 0.5 compare_and_fusion
  20.4 11.5 %multiply_reduce_fusion.2 = (f32[128]{0:T(128)S(1)}, f32[128,1024]{1,0:T(8,128)S(1)}) fusion(bf16[15,1024]{1,0:T(8,128)(2,1)S(1)} %collective-permute-done.1, bf16[128,1024]{1,0:T(8,128)(2,1)} %bitcast.181, f32[1024]{0:T(1024)S(1)} %bitcast.212, f32[1024]{0:T(1024)S(1)} %bitcast.214, f32[1024]{0:T(1024)S(1)} %bitcast.218, f32[1024]{0:T(1024)S(1)} %bitcast.220, ...), kind=kLoop, calls=%fused_computation.260 | loop fusion | flops 24248192 | bytes 975360 | tf_op jit(solution)/shard_map/reduce_sum | solution.py:50
  32.1 0.6 copy-done.3
  32.7 0.8 multiply_convert_fusion.2
  33.5 0.3 broadcast_in_dim.28
  33.8 0.2 reshape.199
  34.0 0.4 convolution_convert_fusion.3
  34.5 0.5 broadcast_in_dim.29
  35.2 108.9 %all_to_all.20 = bf16[128,16,1024]{2,1,0:T(8,128)(2,1)} all-to-all(bf16[128,16,1024]{2,1,0:T(8,128)(2,1)S(1)} %bitcast.179), channel_id=1, replica_groups=mesh['seq'=128,'dp'=2] {'seq'}, dimensions={0} | all-to-all | bytes 8388608 | tf_op jit(solution)/shard_map/all_to_all | solution.py:142
  144.1 4.5 fusion.6
  148.7 4.4 convolution_convert_fusion.1
  153.1 9.8 %all-to-all-start.1 = ((bf16[128,16,1024]{2,1,0:T(8,128)(2,1)}), bf16[128,16,1024]{2,1,0:T(8,128)(2,1)}, u32[]{:S(2)}, u32[]{:S(2)}) async-start(bf16[128,16,1024]{2,1,0:T(8,128)(2,1)} %bitcast.191), calls=%async_computation.1 | async-start | bytes 8388608 | tf_op jit(solution)/shard_map/all_to_all | solution.py:90
  163.0 0.6 pad_clamp_fusion
  163.6 0.7 fusion.2
  164.3 92.5 %all-to-all-done.1 = bf16[128,16,1024]{2,1,0:T(8,128)(2,1)} async-done(((bf16[128,16,1024]{2,1,0:T(8,128)(2,1)}), bf16[128,16,1024]{2,1,0:T(8,128)(2,1)}, u32[]{:S(2)}, u32[]{:S(2)}) %all-to-all-start.1) | async-done | bytes 4194336 | tf_op jit(solution)/shard_map/all_to_all | solution.py:90
  256.8 3.4 convert_reduce_fusion.1
  260.2 2.2 gather_fusion
  262.3 1.4 broadcast_select_fusion.1
  263.7 1.6 reshape.207
  265.3 2.4 fusion.155
  267.7 1.2 fusion.76
  268.9 1.3 multiply_multiply_fusion.1
  270.2 1.1 fusion.73
  271.4 0.5 copy.20
  271.9 1.0 convert_element_type.349
  272.9 1.5 convolution_convert_fusion.2
  274.4 0.5 broadcast_in_dim.31
  275.0 103.7 %all_to_all.21 = bf16[128,16,1024]{2,1,0:T(8,128)(2,1)S(1)} all-to-all(bf16[128,16,1024]{2,1,0:T(8,128)(2,1)S(1)} %bitcast.180), channel_id=1, replica_groups=mesh['seq'=128,'dp'=2] {'seq'}, dimensions={0} | all-to-all | bytes 8388608 | tf_op jit(solution)/shard_map/all_to_all | solution.py:157
  378.7 3.6 multiply_convert_fusion
  382.3 4.3 convolution_convert_fusion
  386.7 9.8 %all-to-all-start.3 = ((bf16[128,16,1024]{2,1,0:T(8,128)(2,1)}), bf16[128,16,1024]{2,1,0:T(8,128)(2,1)}, u32[]{:S(2)}, u32[]{:S(2)}) async-start(bf16[128,16,1024]{2,1,0:T(8,128)(2,1)} %bitcast.188), calls=%async_computation.3 | async-start | bytes 8388608 | tf_op jit(solution)/shard_map/all_to_all | solution.py:171
  396.5 5.7 fusion
  402.2 5.6 fusion.1
  407.8 0.3 all-reduce.5.cloned.1.call-start
  408.1 0.8 fusion.146
  408.9 99.1 %all-reduce.7.cloned.1.call-done = (bf16[1,1024,512]{2,1,0:T(8,128)(2,1)}, bf16[1,512,1024]{2,1,0:T(8,128)(2,1)}) async-done(((bf16[1,1024,512]{2,1,0:T(8,128)(2,1)}, bf16[1,512,1024]{2,1,0:T(8,128)(2,1)}), (bf16[1,1024,512]{2,1,0:T(8,128)(2,1)}, bf16[1,512,1024]{2,1,0:T(8,128)(2,1)})) %all-reduce.7.cloned.1.call-update) | async-done | bytes 2097168 | tf_op jit(solution)/shard_map/psum | solution.py:193
  508.0 2.8 broadcast_in_dim.35
  510.8 2.8 broadcast_in_dim.37
  513.6 3.4 convert_reduce_fusion
  517.0 2.3 gather_fusion.1
  519.4 1.4 broadcast_select_fusion
  520.8 1.6 reshape.215
  522.5 2.5 reduce_sum.386
  525.0 0.3 convolution_add_fusion
  525.5 1.1 multiply_reduce_fusion
  526.7 0.8 fusion.72
  527.5 0.6 fusion.58
  528.1 3.3 collective-permute-start.2
  531.4 1.9 collective-permute-start.3
  533.3 0.7 fusion.52
  534.0 0.5 fusion.43
  534.5 2.7 stack.134
  537.2 77.1 %psum.36 = f32[1024]{0:T(1024)} all-reduce(f32[1024]{0:T(1024)S(1)} %get-tuple-element.8), channel_id=1, replica_groups=mesh['seq'=128,'dp'=2] {'seq','dp'}, use_global_device_ids=true, to_apply=%region_44.46 | all-reduce | flops 1024 | bytes 8192 | tf_op jit(solution)/shard_map/psum | solution.py:189
  614.7 2.8 fusion.141
  617.4 172.9 %all-reduce.5.cloned.1.call-done = (f32[31,1024]{1,0:T(8,128)}, f32[1024,32]{0,1:T(8,128)}) async-done(((f32[31,1024]{1,0:T(8,128)}, f32[1024,32]{0,1:T(8,128)}), (f32[31,1024]{1,0:T(8,128)}, f32[1024,32]{0,1:T(8,128)})) %all-reduce.5.cloned.1.call-update) | async-done | bytes 258064 | tf_op jit(solution)/shard_map/psum | solution.py:189
  790.3 1.6 copy.43
  791.9 1.6 copy.44
  (200 shorter events, 1.3 us)
Async XLA Ops:
  8.0 140.7 %copy-start = (bf16[1,512,1024]{2,1,0:T(8,128)(2,1)S(1)}, bf16[1,512,1024]{2,1,0:T(8,128)(2,1)}, u32[]{:S(2)}) copy-start(bf16[1,512,1024]{2,1,0:T(8,128)(2,1)} %param.16) | copy-start | bytes 3145732
  8.9 11.5 %collective-permute-start = (bf16[15,1024]{1,0:T(8,128)(2,1)S(1)}, bf16[15,1024]{1,0:T(8,128)(2,1)S(1)}, u32[]{:S(2)}, u32[]{:S(2)}) collective-permute-start(bf16[15,1024]{1,0:T(8,128)(2,1)S(1)} %get-tuple-element.62), channel_id=1, source_target_pairs={{0,2},{2,4},{4,6},{6,8},{8,10},{10,12},{12,14},{14,16},{16,18},{18... | collective-permute-start | bytes 92168 | tf_op jit(solution)/shard_map/ppermute | solution.py:16
  13.4 7.0 collective-permute-start.1
  17.4 17.6 %copy-start.10 = (f32[1,1024]{1,0:T(1,128)}, f32[1,1024]{1,0:T(1,128)S(1)}, u32[]{:S(2)}) copy-start(f32[1,1024]{1,0:T(1,128)S(1)} %get-tuple-element.87) | copy-start | bytes 12292
  17.4 17.6 %copy-start.12 = (f32[1,1024]{1,0:T(1,128)}, f32[1,1024]{1,0:T(1,128)S(1)}, u32[]{:S(2)}) copy-start(f32[1,1024]{1,0:T(1,128)S(1)} %get-tuple-element.88) | copy-start | bytes 12292
  17.4 17.6 %copy-start.14 = (f32[1,1024]{1,0:T(1,128)}, f32[1,1024]{1,0:T(1,128)S(1)}, u32[]{:S(2)}) copy-start(f32[1,1024]{1,0:T(1,128)S(1)} %get-tuple-element.89) | copy-start | bytes 12292
  17.5 17.6 %copy-start.16 = (f32[1,1024]{1,0:T(1,128)}, f32[1,1024]{1,0:T(1,128)S(1)}, u32[]{:S(2)}) copy-start(f32[1,1024]{1,0:T(1,128)S(1)} %get-tuple-element.90) | copy-start | bytes 12292
  17.5 17.6 %copy-start.18 = (f32[1,1024]{1,0:T(1,128)}, f32[1,1024]{1,0:T(1,128)S(1)}, u32[]{:S(2)}) copy-start(f32[1,1024]{1,0:T(1,128)S(1)} %get-tuple-element.91) | copy-start | bytes 12292
  17.5 17.6 %copy-start.20 = (f32[1,1024]{1,0:T(1,128)}, f32[1,1024]{1,0:T(1,128)S(1)}, u32[]{:S(2)}) copy-start(f32[1,1024]{1,0:T(1,128)S(1)} %get-tuple-element.92) | copy-start | bytes 12292
  17.5 17.6 %copy-start.22 = (f32[1,1024]{1,0:T(1,128)}, f32[1,1024]{1,0:T(1,128)S(1)}, u32[]{:S(2)}) copy-start(f32[1,1024]{1,0:T(1,128)S(1)} %get-tuple-element.93) | copy-start | bytes 12292
  17.5 17.6 %copy-start.24 = (f32[1,1024]{1,0:T(1,128)}, f32[1,1024]{1,0:T(1,128)S(1)}, u32[]{:S(2)}) copy-start(f32[1,1024]{1,0:T(1,128)S(1)} %get-tuple-element.94) | copy-start | bytes 12292
  18.7 13.3 %copy-start.42 = (f32[1,1024]{1,0:T(1,128)}, f32[1,1024]{1,0:T(1,128)S(1)}, u32[]{:S(2)}) copy-start(f32[1,1024]{1,0:T(1,128)S(1)} %get-tuple-element.72) | copy-start | bytes 12292
  18.7 13.3 %copy-start.44 = (f32[1,1024]{1,0:T(1,128)}, f32[1,1024]{1,0:T(1,128)S(1)}, u32[]{:S(2)}) copy-start(f32[1,1024]{1,0:T(1,128)S(1)} %get-tuple-element.73) | copy-start | bytes 12292
  18.7 13.3 %copy-start.46 = (f32[1,1024]{1,0:T(1,128)}, f32[1,1024]{1,0:T(1,128)S(1)}, u32[]{:S(2)}) copy-start(f32[1,1024]{1,0:T(1,128)S(1)} %get-tuple-element.74) | copy-start | bytes 12292
  18.7 13.3 %copy-start.48 = (f32[1,1024]{1,0:T(1,128)}, f32[1,1024]{1,0:T(1,128)S(1)}, u32[]{:S(2)}) copy-start(f32[1,1024]{1,0:T(1,128)S(1)} %get-tuple-element.75) | copy-start | bytes 12292
  18.7 13.3 %copy-start.50 = (f32[1,1024]{1,0:T(1,128)}, f32[1,1024]{1,0:T(1,128)S(1)}, u32[]{:S(2)}) copy-start(f32[1,1024]{1,0:T(1,128)S(1)} %get-tuple-element.76) | copy-start | bytes 12292
  18.8 13.3 %copy-start.52 = (f32[1,1024]{1,0:T(1,128)}, f32[1,1024]{1,0:T(1,128)S(1)}, u32[]{:S(2)}) copy-start(f32[1,1024]{1,0:T(1,128)S(1)} %get-tuple-element.77) | copy-start | bytes 12292
  18.8 13.3 %copy-start.54 = (f32[1,1024]{1,0:T(1,128)}, f32[1,1024]{1,0:T(1,128)S(1)}, u32[]{:S(2)}) copy-start(f32[1,1024]{1,0:T(1,128)S(1)} %get-tuple-element.78) | copy-start | bytes 12292
  18.8 13.3 %copy-start.56 = (f32[1,1024]{1,0:T(1,128)}, f32[1,1024]{1,0:T(1,128)S(1)}, u32[]{:S(2)}) copy-start(f32[1,1024]{1,0:T(1,128)S(1)} %get-tuple-element.79) | copy-start | bytes 12292
  18.8 16.3 %copy-start.26 = (f32[1,1024]{1,0:T(1,128)}, f32[1,1024]{1,0:T(1,128)S(1)}, u32[]{:S(2)}) copy-start(f32[1,1024]{1,0:T(1,128)S(1)} %get-tuple-element.64) | copy-start | bytes 12292
  18.8 16.3 %copy-start.28 = (f32[1,1024]{1,0:T(1,128)}, f32[1,1024]{1,0:T(1,128)S(1)}, u32[]{:S(2)}) copy-start(f32[1,1024]{1,0:T(1,128)S(1)} %get-tuple-element.65) | copy-start | bytes 12292
  18.8 16.3 %copy-start.30 = (f32[1,1024]{1,0:T(1,128)}, f32[1,1024]{1,0:T(1,128)S(1)}, u32[]{:S(2)}) copy-start(f32[1,1024]{1,0:T(1,128)S(1)} %get-tuple-element.66) | copy-start | bytes 12292
  18.8 16.3 %copy-start.32 = (f32[1,1024]{1,0:T(1,128)}, f32[1,1024]{1,0:T(1,128)S(1)}, u32[]{:S(2)}) copy-start(f32[1,1024]{1,0:T(1,128)S(1)} %get-tuple-element.67) | copy-start | bytes 12292
  18.9 16.3 %copy-start.34 = (f32[1,1024]{1,0:T(1,128)}, f32[1,1024]{1,0:T(1,128)S(1)}, u32[]{:S(2)}) copy-start(f32[1,1024]{1,0:T(1,128)S(1)} %get-tuple-element.68) | copy-start | bytes 12292
  18.9 16.3 %copy-start.36 = (f32[1,1024]{1,0:T(1,128)}, f32[1,1024]{1,0:T(1,128)S(1)}, u32[]{:S(2)}) copy-start(f32[1,1024]{1,0:T(1,128)S(1)} %get-tuple-element.69) | copy-start | bytes 12292
  18.9 16.3 %copy-start.38 = (f32[1,1024]{1,0:T(1,128)}, f32[1,1024]{1,0:T(1,128)S(1)}, u32[]{:S(2)}) copy-start(f32[1,1024]{1,0:T(1,128)S(1)} %get-tuple-element.70) | copy-start | bytes 12292
  18.9 16.3 %copy-start.40 = (f32[1,1024]{1,0:T(1,128)}, f32[1,1024]{1,0:T(1,128)S(1)}, u32[]{:S(2)}) copy-start(f32[1,1024]{1,0:T(1,128)S(1)} %get-tuple-element.71) | copy-start | bytes 12292
  20.4 142.6 %copy-start.64 = (s32[256]{0:T(256)}, s32[256]{0:T(256)S(1)}, u32[]{:S(2)}) copy-start(s32[256]{0:T(256)S(1)} %get-tuple-element.51) | copy-start | bytes 3076
  35.2 108.9 %copy-start.83 = (bf16[1,1024,512]{2,1,0:T(8,128)(2,1)S(1)}, bf16[1,1024,512]{2,1,0:T(8,128)(2,1)}, u32[]{:S(2)}) copy-start(bf16[1,1024,512]{2,1,0:T(8,128)(2,1)} %param.15) | copy-start | bytes 3145732
  153.1 103.7 %all-to-all-start.1 = ((bf16[128,16,1024]{2,1,0:T(8,128)(2,1)}), bf16[128,16,1024]{2,1,0:T(8,128)(2,1)}, u32[]{:S(2)}, u32[]{:S(2)}) async-start(bf16[128,16,1024]{2,1,0:T(8,128)(2,1)} %bitcast.191), calls=%async_computation.1 | async-start | bytes 8388608 | tf_op jit(solution)/shard_map/all_to_all | solution.py:90
  274.9 103.8 %copy-start.88 = (f32[2048,512]{1,0:T(8,128)S(1)}, f32[2048,512]{1,0:T(8,128)}, u32[]{:S(2)}) copy-start(f32[2048,512]{1,0:T(8,128)} %copy-done.87) | copy-start | bytes 12582916
  386.7 126.9 %all-to-all-start.3 = ((bf16[128,16,1024]{2,1,0:T(8,128)(2,1)}), bf16[128,16,1024]{2,1,0:T(8,128)(2,1)}, u32[]{:S(2)}, u32[]{:S(2)}) async-start(bf16[128,16,1024]{2,1,0:T(8,128)(2,1)} %bitcast.188), calls=%async_computation.3 | async-start | bytes 8388608 | tf_op jit(solution)/shard_map/all_to_all | solution.py:171
  396.4 111.5 %all-reduce.7.cloned.1.call-start = ((), (), s32[]{:S(2)}) async-start(), calls=%async_computation.5 | async-start | bytes 4194304 | tf_op jit(solution)/shard_map/psum | solution.py:193
  407.8 382.5 %all-reduce.5.cloned.1.call-start = ((), (), s32[]{:S(2)}) async-start(), calls=%async_computation.4 | async-start | bytes 524288 | tf_op jit(solution)/shard_map/psum | solution.py:189
  525.3 89.1 %copy-start.11 = (f32[1,1024]{1,0:T(1,128)S(1)}, f32[1,1024]{1,0:T(1,128)}, u32[]{:S(2)}) copy-start(f32[1,1024]{1,0:T(1,128)} %copy-done.10) | copy-start | bytes 12292
  525.3 89.1 %copy-start.13 = (f32[1,1024]{1,0:T(1,128)S(1)}, f32[1,1024]{1,0:T(1,128)}, u32[]{:S(2)}) copy-start(f32[1,1024]{1,0:T(1,128)} %copy-done.12) | copy-start | bytes 12292
  525.3 89.1 %copy-start.15 = (f32[1,1024]{1,0:T(1,128)S(1)}, f32[1,1024]{1,0:T(1,128)}, u32[]{:S(2)}) copy-start(f32[1,1024]{1,0:T(1,128)} %copy-done.14) | copy-start | bytes 12292
  525.3 89.1 %copy-start.17 = (f32[1,1024]{1,0:T(1,128)S(1)}, f32[1,1024]{1,0:T(1,128)}, u32[]{:S(2)}) copy-start(f32[1,1024]{1,0:T(1,128)} %copy-done.16) | copy-start | bytes 12292
  525.3 89.1 %copy-start.19 = (f32[1,1024]{1,0:T(1,128)S(1)}, f32[1,1024]{1,0:T(1,128)}, u32[]{:S(2)}) copy-start(f32[1,1024]{1,0:T(1,128)} %copy-done.18) | copy-start | bytes 12292
  525.3 89.1 %copy-start.21 = (f32[1,1024]{1,0:T(1,128)S(1)}, f32[1,1024]{1,0:T(1,128)}, u32[]{:S(2)}) copy-start(f32[1,1024]{1,0:T(1,128)} %copy-done.20) | copy-start | bytes 12292
  525.3 89.1 %copy-start.23 = (f32[1,1024]{1,0:T(1,128)S(1)}, f32[1,1024]{1,0:T(1,128)}, u32[]{:S(2)}) copy-start(f32[1,1024]{1,0:T(1,128)} %copy-done.22) | copy-start | bytes 12292
  525.3 89.1 %copy-start.25 = (f32[1,1024]{1,0:T(1,128)S(1)}, f32[1,1024]{1,0:T(1,128)}, u32[]{:S(2)}) copy-start(f32[1,1024]{1,0:T(1,128)} %copy-done.24) | copy-start | bytes 12292
  525.4 89.1 %copy-start.27 = (f32[1,1024]{1,0:T(1,128)S(1)}, f32[1,1024]{1,0:T(1,128)}, u32[]{:S(2)}) copy-start(f32[1,1024]{1,0:T(1,128)} %copy-done.26) | copy-start | bytes 12292
  525.4 89.1 %copy-start.29 = (f32[1,1024]{1,0:T(1,128)S(1)}, f32[1,1024]{1,0:T(1,128)}, u32[]{:S(2)}) copy-start(f32[1,1024]{1,0:T(1,128)} %copy-done.28) | copy-start | bytes 12292
  525.4 89.1 %copy-start.31 = (f32[1,1024]{1,0:T(1,128)S(1)}, f32[1,1024]{1,0:T(1,128)}, u32[]{:S(2)}) copy-start(f32[1,1024]{1,0:T(1,128)} %copy-done.30) | copy-start | bytes 12292
  525.4 89.1 %copy-start.33 = (f32[1,1024]{1,0:T(1,128)S(1)}, f32[1,1024]{1,0:T(1,128)}, u32[]{:S(2)}) copy-start(f32[1,1024]{1,0:T(1,128)} %copy-done.32) | copy-start | bytes 12292
  525.4 89.1 %copy-start.35 = (f32[1,1024]{1,0:T(1,128)S(1)}, f32[1,1024]{1,0:T(1,128)}, u32[]{:S(2)}) copy-start(f32[1,1024]{1,0:T(1,128)} %copy-done.34) | copy-start | bytes 12292
  525.4 89.1 %copy-start.37 = (f32[1,1024]{1,0:T(1,128)S(1)}, f32[1,1024]{1,0:T(1,128)}, u32[]{:S(2)}) copy-start(f32[1,1024]{1,0:T(1,128)} %copy-done.36) | copy-start | bytes 12292
  525.4 89.1 %copy-start.39 = (f32[1,1024]{1,0:T(1,128)S(1)}, f32[1,1024]{1,0:T(1,128)}, u32[]{:S(2)}) copy-start(f32[1,1024]{1,0:T(1,128)} %copy-done.38) | copy-start | bytes 12292
  525.4 89.1 %copy-start.41 = (f32[1,1024]{1,0:T(1,128)S(1)}, f32[1,1024]{1,0:T(1,128)}, u32[]{:S(2)}) copy-start(f32[1,1024]{1,0:T(1,128)} %copy-done.40) | copy-start | bytes 12292
  525.4 89.1 %copy-start.43 = (f32[1,1024]{1,0:T(1,128)S(1)}, f32[1,1024]{1,0:T(1,128)}, u32[]{:S(2)}) copy-start(f32[1,1024]{1,0:T(1,128)} %copy-done.42) | copy-start | bytes 12292
  525.4 89.1 %copy-start.45 = (f32[1,1024]{1,0:T(1,128)S(1)}, f32[1,1024]{1,0:T(1,128)}, u32[]{:S(2)}) copy-start(f32[1,1024]{1,0:T(1,128)} %copy-done.44) | copy-start | bytes 12292
  525.5 89.1 %copy-start.47 = (f32[1,1024]{1,0:T(1,128)S(1)}, f32[1,1024]{1,0:T(1,128)}, u32[]{:S(2)}) copy-start(f32[1,1024]{1,0:T(1,128)} %copy-done.46) | copy-start | bytes 12292
  525.5 89.1 %copy-start.49 = (f32[1,1024]{1,0:T(1,128)S(1)}, f32[1,1024]{1,0:T(1,128)}, u32[]{:S(2)}) copy-start(f32[1,1024]{1,0:T(1,128)} %copy-done.48) | copy-start | bytes 12292
  525.5 89.1 %copy-start.51 = (f32[1,1024]{1,0:T(1,128)S(1)}, f32[1,1024]{1,0:T(1,128)}, u32[]{:S(2)}) copy-start(f32[1,1024]{1,0:T(1,128)} %copy-done.50) | copy-start | bytes 12292
  525.5 89.1 %copy-start.53 = (f32[1,1024]{1,0:T(1,128)S(1)}, f32[1,1024]{1,0:T(1,128)}, u32[]{:S(2)}) copy-start(f32[1,1024]{1,0:T(1,128)} %copy-done.52) | copy-start | bytes 12292
  525.5 89.1 %copy-start.55 = (f32[1,1024]{1,0:T(1,128)S(1)}, f32[1,1024]{1,0:T(1,128)}, u32[]{:S(2)}) copy-start(f32[1,1024]{1,0:T(1,128)} %copy-done.54) | copy-start | bytes 12292
  525.5 89.1 %copy-start.57 = (f32[1,1024]{1,0:T(1,128)S(1)}, f32[1,1024]{1,0:T(1,128)}, u32[]{:S(2)}) copy-start(f32[1,1024]{1,0:T(1,128)} %copy-done.56) | copy-start | bytes 12292
  525.5 89.1 %copy-start.59 = (f32[1,1024]{1,0:T(1,128)S(1)}, f32[1,1024]{1,0:T(1,128)}, u32[]{:S(2)}) copy-start(f32[1,1024]{1,0:T(1,128)} %copy-done.58) | copy-start | bytes 12292
  525.5 89.1 %copy-start.61 = (f32[1,1024]{1,0:T(1,128)S(1)}, f32[1,1024]{1,0:T(1,128)}, u32[]{:S(2)}) copy-start(f32[1,1024]{1,0:T(1,128)} %copy-done.60) | copy-start | bytes 12292
  525.5 89.1 %copy-start.63 = (f32[1,1024]{1,0:T(1,128)S(1)}, f32[1,1024]{1,0:T(1,128)}, u32[]{:S(2)}) copy-start(f32[1,1024]{1,0:T(1,128)} %copy-done.62) | copy-start | bytes 12292
  528.1 86.2 %collective-permute-start.2 = (bf16[15,1024]{1,0:T(8,128)(2,1)S(1)}, bf16[15,1024]{1,0:T(8,128)(2,1)S(1)}, u32[]{:S(2)}, u32[]{:S(2)}) collective-permute-start(bf16[15,1024]{1,0:T(8,128)(2,1)S(1)} %get-tuple-element.58), channel_id=1, source_target_pairs={{0,2},{2,4},{4,6},{6,8},{8,10},{10,12},{12,14},{14,16},{16,18},{18... | collective-permute-start | bytes 92168 | tf_op jit(solution)/shard_map/ppermute | solution.py:16
  531.4 82.9 %collective-permute-start.3 = (bf16[15,1024]{1,0:T(8,128)(2,1)S(1)}, bf16[15,1024]{1,0:T(8,128)(2,1)S(1)}, u32[]{:S(2)}, u32[]{:S(2)}) collective-permute-start(bf16[15,1024]{1,0:T(8,128)(2,1)S(1)} %get-tuple-element.59), channel_id=1, source_target_pairs={{2,0},{4,2},{6,4},{8,6},{10,8},{12,10},{14,12},{16,14},{18,16},{20... | collective-permute-start | bytes 92168 | tf_op jit(solution)/shard_map/ppermute | solution.py:17
  614.7 178.8 %copy-start.1 = (bf16[1,512,1024]{2,1,0:T(8,128)(2,1)S(1)}, bf16[1,512,1024]{2,1,0:T(8,128)(2,1)}, u32[]{:S(2)}) copy-start(bf16[1,512,1024]{2,1,0:T(8,128)(2,1)} %param.16) | copy-start | bytes 3145732
  (33 other events, 186.6 us)
Sparse Core Ops, SparseCore 0:
  407.9 100.0 all-reduce.6
Sparse Core Ops, SparseCore 1:
  537.2 253.0 all-reduce.4
where the time goes:
time: 811 us; the launch traced here: 801 us
  waiting for transfers between devices  364 us (45%)
  blocking collectives  290 us (36%)
  other arithmetic  44.1 us (5%)
  matrix products  31.9 us (4%)
  starting transfers between devices  31.5 us (4%)
  local copies, waits for them, and re-layouts  22.1 us (3%)
  between operations  17.2 us (2%)
    psum x1, waiting for transfers between devices, body(): lax.psum((kernel_term, gain_term, router_term), ('seq', 'dp'))  173 us
    all_to_all x1, blocking collectives, body(): lax.all_to_all(spread(repeated), 'seq', split_axis=0, concat_axis=0, tile...  109 us
    all_to_all x1, blocking collectives, body(): lax.all_to_all(spread(grad_values), 'seq', split_axis=0, concat_axis=0, t...  104 us
    psum x1, waiting for transfers between devices, body(): lax.psum(in_term.astype(jnp.bfloat16), 'dp').astype(jnp.float32)  99.1 us
    all_to_all x1, waiting for transfers between devices, combine_back(): lax.all_to_all(partial_rows, 'seq', split_axis=0, concat_axis=0, tiled=True)  92.5 us
    psum x1, blocking collectives, body(): lax.psum((kernel_term, gain_term, router_term), ('seq', 'dp'))  77.1 us
  transfers between devices with their start and end apart: 8, of which 3 were waited for; matrix products, arithmetic and copies ran while one was open for 4% of the time, Pallas kernels for 0%

commit v1 on v0

v1 whole, which is shorter than its diff:
```python
import jax
import jax.numpy as jnp
from jax import lax
from jax.sharding import Mesh
from jax.sharding import PartitionSpec as P

eps = 1e-06

SEQ = ("z", "y", "xl", "c")
GRP = ("z", "y")


def padded_2(shard, axis, size, width):
    length = shard.shape[0]
    up = [(i, (i + 1) % size) for i in range(size - 1)]
    down = [(j, i) for i, j in up]
    last = lax.slice_in_dim(shard, length - width, length, axis=0)
    initial = lax.slice_in_dim(shard, 0, width, axis=0)
    before = lax.ppermute(last, axis, up)
    after = lax.ppermute(initial, axis, down)
    return jnp.concatenate([before, shard, after], axis=0)


def conv_forward(padded, kernel, row_count):
    summed = jnp.zeros((row_count, padded.shape[1]), jnp.float32)
    for offset in range(kernel.shape[0]):
        summed = summed + kernel[offset].astype(jnp.float32) * padded[
            offset : offset + row_count
        ].astype(jnp.float32)
    return summed


def conv_transpose(padded, kernel, row_count):
    length = kernel.shape[0]
    summed = jnp.zeros((row_count, padded.shape[1]), jnp.float32)
    for offset in range(length):
        start = length - 1 - offset
        summed = summed + kernel[offset].astype(jnp.float32) * padded[start : start + row_count]
    return summed


def kernel_terms(padded, upstream, length, row_count):
    return jnp.stack(
        [
            jnp.sum(padded[offset : offset + row_count].astype(jnp.float32) * upstream, axis=0)
            for offset in range(length)
        ]
    )


def normalize(summed, norm_gain):
    square = jnp.mean(summed * summed, axis=-1, keepdims=True)
    return summed * lax.rsqrt(square + eps) * norm_gain


def slot_numbers(expert_ids, expert_count):
    onehot = (expert_ids[:, None] == jnp.arange(expert_count, dtype=jnp.int32)[None, :]).astype(
        jnp.int32
    )
    ranks = jnp.cumsum(onehot, axis=0) - onehot
    return jnp.sum(ranks * onehot, axis=1)


def gate_values(normed_b, router, first_ids, second_ids):
    logits = jnp.dot(normed_b, router, preferred_element_type=jnp.float32)
    columns = jnp.arange(router.shape[1], dtype=jnp.int32)[None, :]
    pick_diff = (first_ids[:, None] == columns).astype(jnp.float32) - (
        second_ids[:, None] == columns
    ).astype(jnp.float32)
    gate_one = jax.nn.sigmoid(jnp.sum(logits * pick_diff, axis=1))
    return (gate_one, 1.0 - gate_one, pick_diff)


def swish_parts(pre_act):
    squash = jax.nn.sigmoid(pre_act)
    return (pre_act * squash, squash * (1.0 + pre_act * (1.0 - squash)))


def gate_backward(upstream, out_one, out_two, gate_one, gate_two, pick_diff, normed_b, router):
    grad_gap = (
        (jnp.sum(upstream * out_one, axis=1) - jnp.sum(upstream * out_two, axis=1))
        * gate_one
        * gate_two
    )
    grad_logits = (grad_gap[:, None] * pick_diff).astype(jnp.bfloat16)
    router_term = jnp.dot(normed_b.T, grad_logits, preferred_element_type=jnp.float32)
    normed_term = jnp.dot(grad_logits, router.T, preferred_element_type=jnp.float32)
    return (router_term, normed_term)


def body(frames, kernel, norm_gain, router, experts, w_in, w_out, cotangent):
    inputs_dev = frames[0]
    row_count = inputs_dev.shape[0]
    width = inputs_dev.shape[1]
    length = kernel.shape[0]
    half_width = length // 2
    expert_count = router.shape[1]
    top_count = experts.shape[2]
    capacity = 2 * row_count * top_count // expert_count
    seq_size = lax.psum(1, SEQ)
    in_weights = w_in[0]
    out_weights = w_out[0]
    padded = padded_2(inputs_dev, SEQ, seq_size, half_width)
    summed = inputs_dev.astype(jnp.float32) + conv_forward(padded, kernel, row_count)
    normed_b = normalize(summed, norm_gain).astype(jnp.bfloat16)
    choice_ids = experts[0]
    gate_one, gate_two, pick_diff = gate_values(
        normed_b, router, choice_ids[:, 0], choice_ids[:, 1]
    )
    flat_ids = choice_ids.reshape(-1)
    slot_index = slot_numbers(flat_ids, expert_count)
    position = flat_ids * capacity + slot_index
    dispatch_table = (
        lax.broadcasted_iota(jnp.int32, (expert_count * capacity, flat_ids.shape[0]), 0)
        == position[None, :]
    ).astype(jnp.bfloat16)

    upstream = cotangent[0].astype(jnp.float32)
    repeated = jnp.repeat(normed_b, top_count, axis=0)
    grad_assigned = jnp.stack([gate_one[:, None] * upstream, gate_two[:, None] * upstream], axis=1)
    grad_values = grad_assigned.reshape(row_count * top_count, width).astype(jnp.bfloat16)
    both = jnp.concatenate([repeated, grad_values], axis=1)
    packed = jnp.dot(dispatch_table, both, preferred_element_type=jnp.float32).astype(jnp.bfloat16)
    packed = packed.reshape(expert_count, capacity, 2 * width)
    arrived = lax.all_to_all(packed, GRP, split_axis=0, concat_axis=0, tiled=True)
    arrived = lax.all_gather(arrived, "xl", axis=0, tiled=False)
    arrived = lax.all_gather(arrived, "c", axis=0, tiled=False)
    rows_shape = arrived.shape
    flat = arrived.reshape(-1, 2 * width)
    flat_rows = flat[:, :width]
    flat_grads = flat[:, width:]

    pre_act = jnp.dot(flat_rows, in_weights, preferred_element_type=jnp.float32)
    hidden_f, slope = swish_parts(pre_act)
    hidden = hidden_f.astype(jnp.bfloat16)
    partial_rows = jnp.dot(hidden, out_weights, preferred_element_type=jnp.float32).astype(
        jnp.bfloat16
    )
    grad_hidden = jnp.dot(flat_grads, out_weights.T, preferred_element_type=jnp.float32)
    grad_pre = (grad_hidden * slope).astype(jnp.bfloat16)
    out_term = jnp.dot(hidden.T, flat_grads, preferred_element_type=jnp.float32)
    in_term = jnp.dot(flat_rows.T, grad_pre, preferred_element_type=jnp.float32)
    grad_part = jnp.dot(grad_pre, in_weights.T, preferred_element_type=jnp.float32).astype(
        jnp.bfloat16
    )

    dp_pair = [(0, 1), (1, 0)]
    in_mine, out_mine = in_term.astype(jnp.bfloat16), out_term.astype(jnp.bfloat16)
    in_other = lax.ppermute(in_mine, "dp", dp_pair)
    out_other = lax.ppermute(out_mine, "dp", dp_pair)
    dp_first = lax.axis_index("dp") == 0
    in_a = jnp.where(dp_first, in_mine, in_other).astype(jnp.float32)
    in_b = jnp.where(dp_first, in_other, in_mine).astype(jnp.float32)
    out_a = jnp.where(dp_first, out_mine, out_other).astype(jnp.float32)
    out_b = jnp.where(dp_first, out_other, out_mine).astype(jnp.float32)
    grad_in = in_a + in_b
    grad_out = out_a + out_b

    back = jnp.concatenate([partial_rows, grad_part], axis=1).reshape(rows_shape)
    back = lax.psum_scatter(back, "c", scatter_dimension=0, tiled=True)
    back = lax.psum_scatter(back, "xl", scatter_dimension=1, tiled=True)
    back = back.reshape(expert_count, capacity, 2 * width)
    totals = lax.all_to_all(back, GRP, split_axis=0, concat_axis=0, tiled=True)
    totals = totals.reshape(expert_count * capacity, 2 * width)
    picked = jnp.take(totals, position, axis=0).astype(jnp.float32)
    picked = picked.reshape(row_count, top_count, 2 * width)
    out_one = picked[:, 0, :width]
    out_two = picked[:, 1, :width]
    normed_grads = picked[:, 0, width:] + picked[:, 1, width:]

    mixed = (summed + gate_one[:, None] * out_one + gate_two[:, None] * out_two).astype(
        jnp.bfloat16
    )
    router_term, normed_term = gate_backward(
        upstream, out_one, out_two, gate_one, gate_two, pick_diff, normed_b, router
    )
    pullback = jax.vjp(normalize, summed, norm_gain)[1]
    summed_grad, gain_term = pullback(normed_grads + normed_term)
    upstream_total = upstream + summed_grad
    padded_grad = padded_2(
        upstream_total.astype(jnp.bfloat16), SEQ, seq_size, half_width
    ).astype(upstream_total.dtype)
    grad_frames = (upstream_total + conv_transpose(padded_grad, kernel, row_count)).astype(
        jnp.bfloat16
    )
    kernel_term = kernel_terms(padded, upstream_total, length, row_count)
    small = jnp.concatenate([kernel_term, gain_term[None, :], router_term.T], axis=0)
    for axis in ("c", "xl", "y", "z", "dp"):
        small = lax.psum(small, axis)
    grad_kernel = small[:length]
    grad_gain = small[length]
    grad_router = small[length + 1 :].T
    return (
        mixed[None],
        grad_frames[None],
        grad_kernel,
        grad_gain,
        grad_router,
        grad_in[None],
        grad_out[None],
    )


def solution(mesh):
    split_mesh = Mesh(mesh.devices.reshape(8, 4, 2, 2, 2), SEQ + ("dp",))
    return jax.shard_map(
        body,
        mesh=split_mesh,
        in_specs=(
            P("dp", SEQ, None),
            P(),
            P(),
            P(),
            P("dp", SEQ, None),
            P(SEQ, None, None),
            P(SEQ, None, None),
            P("dp", SEQ, None),
        ),
        out_specs=(
            P("dp", SEQ, None),
            P("dp", SEQ, None),
            P(),
            P(),
            P(),
            P(SEQ, None, None),
            P(SEQ, None, None),
        ),
        check_vma=False,
    )
```

time: 811 us -> 621 us (0.77); the launches traced: 801 us -> 620 us
  blocking collectives: 290 us -> 58 us
  waiting for transfers between devices: 364 us -> 423 us
    all_to_all x2 -> x1, blocking collectives: 213 us -> 58 us  [body(): lax.all_to_all(packed, GRP, split_axis=0, concat_axis=0, tiled=True)]
    all_gather x0 -> x2, waiting for transfers between devices: none -> 92.2 us  [the longest x1 63.6 us: body(): arrived = lax.all_gather(arrived, 'xl', axis=0, tiled=False)]
    reduce_scatter x0 -> x2, waiting for transfers between devices: none -> 85.5 us  [the longest x1 62.4 us: body(): back = lax.psum_scatter(back, 'xl', scatter_dimension=1, tiled=True)]
    psum x1 -> x0, blocking collectives: 77.1 us -> none  [body(): lax.psum((kernel_term, gain_term, router_term), ('seq', 'dp'))]
    psum x2 -> x5, waiting for transfers between devices: 272 us -> 208 us  [body(): small = lax.psum(small, axis)]
    all_to_all x2 -> x1, waiting for transfers between devices: 92.5 us -> 38 us  [body(): totals = lax.all_to_all(back, GRP, split_axis=0, concat_axis=0, tiled=True)]
    concatenate x0 -> x2, local copies, waits for them, and re-layouts: none -> 15.6 us  [the longest x1 12.3 us: body(): jnp.concatenate([partial_rows, grad_part], axis=1).reshape(rows_shape)]
    reduce_sum x4 -> x0, other arithmetic: 10.3 us -> none  [the longest x2 6.72 us: slice_totals(): jnp.sum(returned.astype(jnp.float32).reshape(expert_count, group_size, ca...]
  transfers between devices with their start and end apart: 8 -> 16, of which waited for: 3 -> 10; matrix products, arithmetic and copies ran while one was open for 4% -> 6% of each run, Pallas kernels for 0% -> 0%
where the time goes in v1:
time: 621 us; the launch traced here: 620 us
  waiting for transfers between devices  423 us (68%)
  blocking collectives  58 us (9%)
  other arithmetic  36 us (6%)
  matrix products  31.6 us (5%)
  local copies, waits for them, and re-layouts  29.8 us (5%)
  starting transfers between devices  26.8 us (4%)
  between operations  14.8 us (2%)
    psum x5, waiting for transfers between devices, body(): small = lax.psum(small, axis)  208 us
    all_gather x1, waiting for transfers between devices, body(): arrived = lax.all_gather(arrived, 'xl', axis=0, tiled=False)  63.6 us
    reduce_scatter x1, waiting for transfers between devices, body(): back = lax.psum_scatter(back, 'xl', scatter_dimension=1, tiled=True)  62.4 us
    all_to_all x1, blocking collectives, body(): lax.all_to_all(packed, GRP, split_axis=0, concat_axis=0, tiled=True)  58 us
    all_to_all x1, waiting for transfers between devices, body(): totals = lax.all_to_all(back, GRP, split_axis=0, concat_axis=0, tiled=True)  38 us
    all_gather x1, waiting for transfers between devices, body(): arrived = lax.all_gather(arrived, 'c', axis=0, tiled=False)  28.6 us
    reduce_scatter x1, waiting for transfers between devices, body(): back = lax.psum_scatter(back, 'c', scatter_dimension=0, tiled=True)  23.1 us
  transfers between devices with their start and end apart: 16, of which 10 were waited for; matrix products, arithmetic and copies ran while one was open for 6% of the time, Pallas kernels for 0%

profile of v1, /device:TPU:1, one launch (start us, length us, event | category | flops | bytes accessed | tf_op | source)
XLA Modules:
  0.0 620.3 jit_solution(765407525963802871)
XLA Ops:
  7.2 0.9 slice_bitcast_fusion.4
  8.1 4.5 collective-permute-start
  12.6 1.9 collective-permute-start.1
  14.6 0.8 copy.43
  15.5 0.1 eq.75
  15.6 1.0 slice_convert_fusion.29
  16.7 1.2 slice_convert_fusion.30
  18.0 0.6 reduce-window.6
  18.6 0.2 slice_reduce_fusion
  18.9 0.8 slice_bitcast_fusion.6
  19.7 9.2 %multiply_reduce_fusion.2 = (f32[128]{0:T(128)S(1)}, f32[128,1024]{1,0:T(8,128)S(1)}) fusion(bf16[15,1024]{1,0:T(8,128)(2,1)S(1)} %collective-permute-done.1, bf16[128,1024]{1,0:T(8,128)(2,1)} %bitcast.175, f32[1024]{0:T(1024)S(1)} %bitcast.202, f32[1024]{0:T(1024)S(1)} %bitcast.204, f32[1024]{0:T(1024)S(1)} %bitcast.208, f32[1024]{0:T(1024)S(1)} %bitcast.210, ...), kind=kLoop, calls=%fused_computation.269 | loop fusion | flops 24248192 | bytes 975360 | tf_op jit(solution)/shard_map/reduce_sum | solution.py:52
  29.1 0.4 copy-done.44
  29.5 0.3 copy-done.2
  29.8 0.8 multiply_convert_fusion.2
  30.6 1.0 fusion.16
  31.7 0.3 broadcast_in_dim.20
  32.0 0.2 reshape.206
  32.2 0.2 fusion.90
  32.4 0.5 copy.47
  33.0 0.2 convert_element_type.351
  33.2 0.7 convolution_convert_fusion.2
  33.9 58.0 %all_to_all.10 = bf16[32,16,2048]{2,1,0:T(8,128)(2,1)} all-to-all(bf16[32,16,2048]{2,1,0:T(8,128)(2,1)S(1)} %bitcast.174), channel_id=1, replica_groups=mesh['z'=8,'y'=4,'xl'=2,'c'=2,'dp'=2] {'z','y'}, dimensions={0} | all-to-all | bytes 4194304 | tf_op jit(solution)/shard_map/all_to_all | solution.py:125
  92.0 63.6 %all-gather.5.cloned.1.call-done = bf16[64,16,2048]{2,1,0:T(8,128)(2,1)} async-done(((bf16[32,16,2048]{2,1,0:T(8,128)(2,1)}), bf16[64,16,2048]{2,1,0:T(8,128)(2,1)}) %all-gather.5.cloned.1.call-update) | async-done | bytes 4194320 | tf_op jit(solution)/shard_map/all_gather | solution.py:126
  155.6 0.2 reduce-scatter.3.cloned.1.call-start
  155.8 28.6 %all-gather.7.cloned.1.call-done = bf16[4,32,16,2048]{3,2,1,0:T(8,128)(2,1)} async-done(((bf16[2,32,16,2048]{3,2,1,0:T(8,128)(2,1)}), bf16[4,32,16,2048]{3,2,1,0:T(8,128)(2,1)}) %all-gather.7.cloned.1.call-update) | async-done | bytes 8388624 | tf_op jit(solution)/shard_map/all_gather | solution.py:127
  184.5 4.7 fusion.6
  189.2 3.6 multiply_convert_fusion
  192.8 4.5 convolution_convert_fusion.1
  197.3 4.3 convolution_convert_fusion
  201.6 8.3 %pad_maximum_fusion = bf16[2048,2048]{0,1:T(8,128)(2,1)} fusion(bf16[2048,1024]{0,1:T(8,128)(2,1)} %convolution_convert_fusion, bf16[2048,1024]{0,1:T(8,128)(2,1)} %convolution_convert_fusion.1), kind=kLoop, calls=%fused_computation.1 | loop fusion | flops 16777216 | bytes 16777216 | tf_op jit(solution)/shard_map/concatenate | solution.py:159
  210.0 12.3 %copy.48 = bf16[2048,2048]{1,0:T(8,128)(2,1)} copy(bf16[2048,2048]{0,1:T(8,128)(2,1)} %pad_maximum_fusion) | data formatting | bytes 16777216 | tf_op jit(solution)/shard_map/concatenate | solution.py:159
  222.3 23.1 %reduce-scatter.3.cloned.1.call-done = bf16[1,2,32,16,2048]{4,3,2,1,0:T(8,128)(2,1)} async-done(((bf16[2,2,32,16,2048]{4,3,2,1,0:T(8,128)(2,1)}), bf16[1,2,32,16,2048]{4,3,2,1,0:T(8,128)(2,1)}) %reduce-scatter.3.cloned.1.call-update) | async-done | bytes 4194320 | tf_op jit(solution)/shard_map/reduce_scatter | solution.py:160
  245.4 62.4 %reduce-scatter.5.cloned.1.call-done = bf16[1,1,32,16,2048]{4,3,2,1,0:T(8,128)(2,1)} async-done(((bf16[1,2,32,16,2048]{4,3,2,1,0:T(8,128)(2,1)}), bf16[1,1,32,16,2048]{4,3,2,1,0:T(8,128)(2,1)}) %reduce-scatter.5.cloned.1.call-update) | async-done | bytes 2097168 | tf_op jit(solution)/shard_map/reduce_scatter | solution.py:161
  307.8 9.6 %all-to-all-start.1 = ((bf16[32,16,2048]{2,1,0:T(8,128)(2,1)}), bf16[32,16,2048]{2,1,0:T(8,128)(2,1)S(1)}, u32[]{:S(2)}, u32[]{:S(2)}) async-start(bf16[32,16,2048]{2,1,0:T(8,128)(2,1)} %bitcast.181), calls=%async_computation.3 | async-start | bytes 4194304 | tf_op jit(solution)/shard_map/all_to_all | solution.py:163
  318.0 0.5 compare_and_fusion
  318.5 6.9 %fusion.11 = bf16[512,1024]{1,0:T(8,128)(2,1)} fusion(bf16[2048,2048]{1,0:T(8,128)(2,1)} %bitcast.281, f32[2048,512]{1,0:T(8,128)} %copy-done.48), kind=kOutput, calls=%fused_computation.47 | convolution fusion | flops 2153250816 | bytes 9437184 | tf_op jit(solution)/shard_map/dot_general | solution.py:141
  325.5 2.4 collective-permute-start.5
  327.8 38.0 %all-to-all-done.1 = bf16[32,16,2048]{2,1,0:T(8,128)(2,1)S(1)} async-done(((bf16[32,16,2048]{2,1,0:T(8,128)(2,1)}), bf16[32,16,2048]{2,1,0:T(8,128)(2,1)S(1)}, u32[]{:S(2)}, u32[]{:S(2)}) %all-to-all-start.1) | async-done | bytes 2097184 | tf_op jit(solution)/shard_map/all_to_all | solution.py:163
  365.8 2.3 gather_fusion
  368.2 1.8 gather.7
  370.1 1.3 fusion.24
  371.4 1.0 fusion.93
  372.5 0.4 multiply_reduce_fusion
  372.9 0.2 fusion.163
  373.1 0.8 fusion.89
  374.0 0.5 fusion.60
  374.5 0.7 fusion.69
  375.1 0.6 fusion.75
  375.7 3.3 concatenate.52
  379.1 5.2 fusion.8
  384.3 2.5 collective-permute-start.4
  386.8 21.3 %all-reduce.6.cloned.1.call-done = f32[64,1024]{1,0:T(8,128)} async-done(((f32[64,1024]{1,0:T(8,128)}), f32[64,1024]{1,0:T(8,128)}) %all-reduce.6.cloned.1.call-update) | async-done | bytes 262160 | tf_op jit(solution)/shard_map/psum | solution.py:189
  408.1 37.5 %all-reduce.8.cloned.1.call-done = f32[64,1024]{1,0:T(8,128)} async-done(((f32[64,1024]{1,0:T(8,128)}), f32[64,1024]{1,0:T(8,128)}) %all-reduce.8.cloned.1.call-update) | async-done | bytes 262160 | tf_op jit(solution)/shard_map/psum | solution.py:189
  445.8 3.3 add_bitcast_fusion
  449.1 3.5 collective-permute-start.2
  452.6 1.9 collective-permute-start.3
  454.6 39.8 %all-reduce.10.cloned.1.call-done = f32[64,1024]{1,0:T(8,128)} async-done(((f32[64,1024]{1,0:T(8,128)}), f32[64,1024]{1,0:T(8,128)}) %all-reduce.10.cloned.1.call-update) | async-done | bytes 262160 | tf_op jit(solution)/shard_map/psum | solution.py:189
  494.4 2.9 add_bitcast_fusion.1
  497.4 69.7 %all-reduce.12.cloned.1.call-done = f32[64,1024]{1,0:T(8,128)} async-done(((f32[64,1024]{1,0:T(8,128)}), f32[64,1024]{1,0:T(8,128)}) %all-reduce.12.cloned.1.call-update) | async-done | bytes 262160 | tf_op jit(solution)/shard_map/psum | solution.py:189
  567.3 2.8 fusion.158
  570.1 39.2 %all-reduce.14.cloned.1.call-done = f32[64,1024]{1,0:T(8,128)} async-done(((f32[64,1024]{1,0:T(8,128)}), f32[64,1024]{1,0:T(8,128)}) %all-reduce.14.cloned.1.call-update) | async-done | bytes 262160 | tf_op jit(solution)/shard_map/psum | solution.py:189
  609.3 1.4 slice.634
  610.7 1.6 slice_bitcast_fusion.2
  612.2 1.6 slice.633
  (141 shorter events, 1.7 us)
Async XLA Ops:
  7.2 182.0 %copy-start = (bf16[1,512,1024]{2,1,0:T(8,128)(2,1)S(1)}, bf16[1,512,1024]{2,1,0:T(8,128)(2,1)}, u32[]{:S(2)}) copy-start(bf16[1,512,1024]{2,1,0:T(8,128)(2,1)} %param.14) | copy-start | bytes 3145732
  7.2 25.0 %copy-start.5 = (bf16[1,128,1024]{2,1,0:T(8,128)(2,1)S(1)}, bf16[1,128,1024]{2,1,0:T(8,128)(2,1)}, u32[]{:S(2)}) copy-start(bf16[1,128,1024]{2,1,0:T(8,128)(2,1)} %param.15) | copy-start | bytes 786436
  7.2 148.4 %all-gather.5.cloned.1.call-start = ((), (), s32[]{:S(2)}) async-start(), calls=%async_computation.11 | async-start | bytes 6291456 | tf_op jit(solution)/shard_map/all_gather | solution.py:126
  8.1 11.6 %collective-permute-start = (bf16[15,1024]{1,0:T(8,128)(2,1)S(1)}, bf16[15,1024]{1,0:T(8,128)(2,1)S(1)}, u32[]{:S(2)}, u32[]{:S(2)}) collective-permute-start(bf16[15,1024]{1,0:T(8,128)(2,1)S(1)} %get-tuple-element.53), channel_id=1, source_target_pairs={{0,2},{2,4},{4,6},{6,8},{8,10},{10,12},{12,14},{14,16},{16,18},{18... | collective-permute-start | bytes 92168 | tf_op jit(solution)/shard_map/ppermute | solution.py:19
  12.6 7.1 %collective-permute-start.1 = (bf16[15,1024]{1,0:T(8,128)(2,1)S(1)}, bf16[15,1024]{1,0:T(8,128)(2,1)S(1)}, u32[]{:S(2)}, u32[]{:S(2)}) collective-permute-start(bf16[15,1024]{1,0:T(8,128)(2,1)S(1)} %get-tuple-element.54), channel_id=1, source_target_pairs={{2,0},{4,2},{6,4},{8,6},{10,8},{12,10},{14,12},{16,14},{18,16},{20... | collective-permute-start | bytes 92168 | tf_op jit(solution)/shard_map/ppermute | solution.py:20
  17.9 11.1 %copy-start.9 = (f32[1,1024]{1,0:T(1,128)}, f32[1,1024]{1,0:T(1,128)S(1)}, u32[]{:S(2)}) copy-start(f32[1,1024]{1,0:T(1,128)S(1)} %get-tuple-element.63) | copy-start | bytes 12292
  17.9 11.1 %copy-start.11 = (f32[1,1024]{1,0:T(1,128)}, f32[1,1024]{1,0:T(1,128)S(1)}, u32[]{:S(2)}) copy-start(f32[1,1024]{1,0:T(1,128)S(1)} %get-tuple-element.64) | copy-start | bytes 12292
  17.9 11.1 %copy-start.13 = (f32[1,1024]{1,0:T(1,128)}, f32[1,1024]{1,0:T(1,128)S(1)}, u32[]{:S(2)}) copy-start(f32[1,1024]{1,0:T(1,128)S(1)} %get-tuple-element.65) | copy-start | bytes 12292
  17.9 11.1 %copy-start.15 = (f32[1,1024]{1,0:T(1,128)}, f32[1,1024]{1,0:T(1,128)S(1)}, u32[]{:S(2)}) copy-start(f32[1,1024]{1,0:T(1,128)S(1)} %get-tuple-element.66) | copy-start | bytes 12292
  17.9 11.1 %copy-start.17 = (f32[1,1024]{1,0:T(1,128)}, f32[1,1024]{1,0:T(1,128)S(1)}, u32[]{:S(2)}) copy-start(f32[1,1024]{1,0:T(1,128)S(1)} %get-tuple-element.67) | copy-start | bytes 12292
  17.9 11.1 %copy-start.19 = (f32[1,1024]{1,0:T(1,128)}, f32[1,1024]{1,0:T(1,128)S(1)}, u32[]{:S(2)}) copy-start(f32[1,1024]{1,0:T(1,128)S(1)} %get-tuple-element.68) | copy-start | bytes 12292
  17.9 11.1 %copy-start.21 = (f32[1,1024]{1,0:T(1,128)}, f32[1,1024]{1,0:T(1,128)S(1)}, u32[]{:S(2)}) copy-start(f32[1,1024]{1,0:T(1,128)S(1)} %get-tuple-element.69) | copy-start | bytes 12292
  17.9 11.1 %copy-start.23 = (f32[1,1024]{1,0:T(1,128)}, f32[1,1024]{1,0:T(1,128)S(1)}, u32[]{:S(2)}) copy-start(f32[1,1024]{1,0:T(1,128)S(1)} %get-tuple-element.70) | copy-start | bytes 12292
  18.0 11.1 %copy-start.25 = (f32[1,1024]{1,0:T(1,128)}, f32[1,1024]{1,0:T(1,128)S(1)}, u32[]{:S(2)}) copy-start(f32[1,1024]{1,0:T(1,128)S(1)} %get-tuple-element.71) | copy-start | bytes 12292
  18.0 11.1 %copy-start.27 = (f32[1,1024]{1,0:T(1,128)}, f32[1,1024]{1,0:T(1,128)S(1)}, u32[]{:S(2)}) copy-start(f32[1,1024]{1,0:T(1,128)S(1)} %get-tuple-element.72) | copy-start | bytes 12292
  18.0 11.1 %copy-start.29 = (f32[1,1024]{1,0:T(1,128)}, f32[1,1024]{1,0:T(1,128)S(1)}, u32[]{:S(2)}) copy-start(f32[1,1024]{1,0:T(1,128)S(1)} %get-tuple-element.73) | copy-start | bytes 12292
  18.9 10.2 %copy-start.31 = (s32[256]{0:T(256)}, s32[256]{0:T(256)S(1)}, u32[]{:S(2)}) copy-start(s32[256]{0:T(256)S(1)} %fusion.161) | copy-start | bytes 3076
  19.7 14.2 %copy-start.34 = (s32[128]{0:T(128)}, s32[128]{0:T(128)S(1)}, u32[]{:S(2)}) copy-start(s32[128]{0:T(128)S(1)} %get-tuple-element.86) | copy-start | bytes 1540
  19.7 14.2 %copy-start.36 = (s32[128]{0:T(128)}, s32[128]{0:T(128)S(1)}, u32[]{:S(2)}) copy-start(s32[128]{0:T(128)S(1)} %get-tuple-element.87) | copy-start | bytes 1540
  29.5 1.1 copy-start.40
  31.7 2.2 copy-start.38
  31.7 2.2 copy-start.42
  91.9 92.6 %copy-start.47 = (bf16[1,1024,512]{2,1,0:T(8,128)(2,1)S(1)}, bf16[1,1024,512]{2,1,0:T(8,128)(2,1)}, u32[]{:S(2)}) copy-start(bf16[1,1024,512]{2,1,0:T(8,128)(2,1)} %param.13) | copy-start | bytes 3145732
  91.9 92.5 %all-gather.7.cloned.1.call-start = ((), (), s32[]{:S(2)}) async-start(), calls=%async_computation.12 | async-start | bytes 12582912 | tf_op jit(solution)/shard_map/all_gather | solution.py:127
  155.6 89.8 %reduce-scatter.3.cloned.1.call-start = ((), (), s32[]{:S(2)}) async-start(), calls=%async_computation.4 | async-start | bytes 12582912 | tf_op jit(solution)/shard_map/reduce_scatter | solution.py:160
  184.5 4.7 copy-start.46
  189.2 3.6 copy-start.48
  192.8 4.5 copy-start.49
  222.3 85.5 %reduce-scatter.5.cloned.1.call-start = ((), (), s32[]{:S(2)}) async-start(), calls=%async_computation.5 | async-start | bytes 6291456 | tf_op jit(solution)/shard_map/reduce_scatter | solution.py:161
  245.4 72.1 %copy-start.32 = (s32[256]{0:T(256)S(1)}, s32[256]{0:T(256)}, u32[]{:S(2)}) copy-start(s32[256]{0:T(256)} %copy-done.31) | copy-start | bytes 3076
  245.4 72.2 %copy-start.33 = (s32[1,128,2]{1,2,0:T(2,128)S(1)}, s32[1,128,2]{1,2,0:T(2,128)}, u32[]{:S(2)}) copy-start(s32[1,128,2]{1,2,0:T(2,128)} %param.12) | copy-start | bytes 3076
  307.8 58.0 %all-to-all-start.1 = ((bf16[32,16,2048]{2,1,0:T(8,128)(2,1)}), bf16[32,16,2048]{2,1,0:T(8,128)(2,1)S(1)}, u32[]{:S(2)}, u32[]{:S(2)}) async-start(bf16[32,16,2048]{2,1,0:T(8,128)(2,1)} %bitcast.181), calls=%async_computation.3 | async-start | bytes 4194304 | tf_op jit(solution)/shard_map/all_to_all | solution.py:163
  317.4 90.6 %all-reduce.6.cloned.1.call-start = ((), (), s32[]{:S(2)}) async-start(), calls=%async_computation.6 | async-start | bytes 524288 | tf_op jit(solution)/shard_map/psum | solution.py:189
  325.5 120.4 %collective-permute-start.5 = (bf16[512,1024]{1,0:T(8,128)(2,1)}, bf16[512,1024]{1,0:T(8,128)(2,1)}, u32[]{:S(2)}, u32[]{:S(2)}) collective-permute-start(bf16[512,1024]{1,0:T(8,128)(2,1)} %fusion.11), channel_id=1, source_target_pairs={{0,1},{1,0},{2,3},{3,2},{4,5},{5,4},{6,7},{7,6},{8,9},{9,8},{10,11... | collective-permute-start | bytes 3145736 | tf_op jit(solution)/shard_map/ppermute | solution.py:150
  368.1 3.3 copy-start.3
  368.1 3.3 copy-start.6
  368.1 3.3 copy-start.39
  368.2 3.3 copy-start.43
  368.2 4.3 copy-start.7
  368.2 4.3 copy-start.8
  368.2 4.3 copy-start.35
  368.2 4.3 copy-start.37
  368.2 4.3 copy-start.41
  368.2 4.9 copy-start.45
  368.2 4.9 copy-start.4
  379.0 66.6 %all-reduce.8.cloned.1.call-start = ((), (), s32[]{:S(2)}) async-start(), calls=%async_computation.7 | async-start | bytes 524288 | tf_op jit(solution)/shard_map/psum | solution.py:189
  384.3 110.1 %collective-permute-start.4 = (bf16[1024,512]{1,0:T(8,128)(2,1)S(1)}, bf16[1024,512]{1,0:T(8,128)(2,1)}, u32[]{:S(2)}, u32[]{:S(2)}) collective-permute-start(bf16[1024,512]{1,0:T(8,128)(2,1)S(1)} %fusion.8), channel_id=1, source_target_pairs={{0,1},{1,0},{2,3},{3,2},{4,5},{5,4},{6,7},{7,6},{8,9},{9,8},{10,11... | collective-permute-start | bytes 3145736 | tf_op jit(solution)/shard_map/ppermute | solution.py:149
  408.1 86.3 %all-reduce.10.cloned.1.call-start = ((), (), s32[]{:S(2)}) async-start(), calls=%async_computation.8 | async-start | bytes 524288 | tf_op jit(solution)/shard_map/psum | solution.py:189
  445.7 121.6 %copy-start.10 = (f32[1,1024]{1,0:T(1,128)S(1)}, f32[1,1024]{1,0:T(1,128)}, u32[]{:S(2)}) copy-start(f32[1,1024]{1,0:T(1,128)} %copy-done.9) | copy-start | bytes 12292
  445.7 121.6 %copy-start.12 = (f32[1,1024]{1,0:T(1,128)S(1)}, f32[1,1024]{1,0:T(1,128)}, u32[]{:S(2)}) copy-start(f32[1,1024]{1,0:T(1,128)} %copy-done.11) | copy-start | bytes 12292
  445.7 121.5 %copy-start.14 = (f32[1,1024]{1,0:T(1,128)S(1)}, f32[1,1024]{1,0:T(1,128)}, u32[]{:S(2)}) copy-start(f32[1,1024]{1,0:T(1,128)} %copy-done.13) | copy-start | bytes 12292
  445.7 121.5 %copy-start.16 = (f32[1,1024]{1,0:T(1,128)S(1)}, f32[1,1024]{1,0:T(1,128)}, u32[]{:S(2)}) copy-start(f32[1,1024]{1,0:T(1,128)} %copy-done.15) | copy-start | bytes 12292
  445.7 121.5 %copy-start.18 = (f32[1,1024]{1,0:T(1,128)S(1)}, f32[1,1024]{1,0:T(1,128)}, u32[]{:S(2)}) copy-start(f32[1,1024]{1,0:T(1,128)} %copy-done.17) | copy-start | bytes 12292
  445.7 121.5 %copy-start.20 = (f32[1,1024]{1,0:T(1,128)S(1)}, f32[1,1024]{1,0:T(1,128)}, u32[]{:S(2)}) copy-start(f32[1,1024]{1,0:T(1,128)} %copy-done.19) | copy-start | bytes 12292
  445.7 121.5 %copy-start.22 = (f32[1,1024]{1,0:T(1,128)S(1)}, f32[1,1024]{1,0:T(1,128)}, u32[]{:S(2)}) copy-start(f32[1,1024]{1,0:T(1,128)} %copy-done.21) | copy-start | bytes 12292
  445.7 121.5 %copy-start.24 = (f32[1,1024]{1,0:T(1,128)S(1)}, f32[1,1024]{1,0:T(1,128)}, u32[]{:S(2)}) copy-start(f32[1,1024]{1,0:T(1,128)} %copy-done.23) | copy-start | bytes 12292
  445.7 121.5 %copy-start.26 = (f32[1,1024]{1,0:T(1,128)S(1)}, f32[1,1024]{1,0:T(1,128)}, u32[]{:S(2)}) copy-start(f32[1,1024]{1,0:T(1,128)} %copy-done.25) | copy-start | bytes 12292
  445.7 121.5 %copy-start.28 = (f32[1,1024]{1,0:T(1,128)S(1)}, f32[1,1024]{1,0:T(1,128)}, u32[]{:S(2)}) copy-start(f32[1,1024]{1,0:T(1,128)} %copy-done.27) | copy-start | bytes 12292
  445.8 121.5 %copy-start.30 = (f32[1,1024]{1,0:T(1,128)S(1)}, f32[1,1024]{1,0:T(1,128)}, u32[]{:S(2)}) copy-start(f32[1,1024]{1,0:T(1,128)} %copy-done.29) | copy-start | bytes 12292
  445.8 121.4 %all-reduce.12.cloned.1.call-start = ((), (), s32[]{:S(2)}) async-start(), calls=%async_computation.9 | async-start | bytes 524288 | tf_op jit(solution)/shard_map/psum | solution.py:189
  449.1 48.2 %collective-permute-start.2 = (bf16[15,1024]{1,0:T(8,128)(2,1)S(1)}, bf16[15,1024]{1,0:T(8,128)(2,1)S(1)}, u32[]{:S(2)}, u32[]{:S(2)}) collective-permute-start(bf16[15,1024]{1,0:T(8,128)(2,1)S(1)} %get-tuple-element.49), channel_id=1, source_target_pairs={{0,2},{2,4},{4,6},{6,8},{8,10},{10,12},{12,14},{14,16},{16,18},{18... | collective-permute-start | bytes 92168 | tf_op jit(solution)/shard_map/ppermute | solution.py:19
  452.6 44.7 %collective-permute-start.3 = (bf16[15,1024]{1,0:T(8,128)(2,1)S(1)}, bf16[15,1024]{1,0:T(8,128)(2,1)S(1)}, u32[]{:S(2)}, u32[]{:S(2)}) collective-permute-start(bf16[15,1024]{1,0:T(8,128)(2,1)S(1)} %get-tuple-element.50), channel_id=1, source_target_pairs={{2,0},{4,2},{6,4},{8,6},{10,8},{12,10},{14,12},{16,14},{18,16},{20... | collective-permute-start | bytes 92168 | tf_op jit(solution)/shard_map/ppermute | solution.py:20
  494.4 114.9 %all-reduce.14.cloned.1.call-start = ((), (), s32[]{:S(2)}) async-start(), calls=%async_computation.10 | async-start | bytes 524288 | tf_op jit(solution)/shard_map/psum | solution.py:189
  567.3 46.5 %copy-start.1 = (bf16[1,512,1024]{2,1,0:T(8,128)(2,1)S(1)}, bf16[1,512,1024]{2,1,0:T(8,128)(2,1)}, u32[]{:S(2)}) copy-start(bf16[1,512,1024]{2,1,0:T(8,128)(2,1)} %param.14) | copy-start | bytes 3145732
  (2 other events, 1.4 us)
Sparse Core Ops, SparseCore 0:
  92.1 63.4 all-gather.4
  157.4 27.0 all-gather.6
  222.4 22.9 reduce-scatter.2
  247.8 59.9 reduce-scatter.4
  379.2 28.8 all-reduce.5
  410.5 35.0 all-reduce.7
  447.9 46.3 all-reduce.9
  496.7 70.4 all-reduce.11
  569.8 39.5 all-reduce.13

commit v2 on v1

--- a/solution.py
+++ b/solution.py
@@ -123,29 +123,51 @@
     packed = jnp.dot(dispatch_table, both, preferred_element_type=jnp.float32).astype(jnp.bfloat16)
     packed = packed.reshape(expert_count, capacity, 2 * width)
     arrived = lax.all_to_all(packed, GRP, split_axis=0, concat_axis=0, tiled=True)
-    arrived = lax.all_gather(arrived, "xl", axis=0, tiled=False)
-    arrived = lax.all_gather(arrived, "c", axis=0, tiled=False)
-    rows_shape = arrived.shape
+    in_all = lax.all_gather(lax.all_gather(in_weights, "xl", axis=0), "c", axis=0)
+    out_all = lax.all_gather(lax.all_gather(out_weights, "xl", axis=0), "c", axis=0)
+    slices = in_all.shape[0] * in_all.shape[1]
+    hid = in_weights.shape[1]
+    in_all = in_all.reshape(slices, width, hid)
+    out_all = out_all.reshape(slices, hid, width)
     flat = arrived.reshape(-1, 2 * width)
     flat_rows = flat[:, :width]
     flat_grads = flat[:, width:]
-
-    pre_act = jnp.dot(flat_rows, in_weights, preferred_element_type=jnp.float32)
+    n_rows = flat.shape[0]
+
+    in_cat = jnp.transpose(in_all, (1, 0, 2)).reshape(width, slices * hid)
+    out_cat = out_all.reshape(slices * hid, width)
+    pre_act = jnp.dot(flat_rows, in_cat, preferred_element_type=jnp.float32)
     hidden_f, slope = swish_parts(pre_act)
     hidden = hidden_f.astype(jnp.bfloat16)
-    partial_rows = jnp.dot(hidden, out_weights, preferred_element_type=jnp.float32).astype(
-        jnp.bfloat16
-    )
-    grad_hidden = jnp.dot(flat_grads, out_weights.T, preferred_element_type=jnp.float32)
+    hidden_s = hidden.reshape(n_rows, slices, hid)
+    partial_rows = jnp.einsum(
+        "rsh,shd->srd", hidden_s, out_all, preferred_element_type=jnp.float32
+    ).astype(jnp.bfloat16)
+    expert_rows = partial_rows[0].astype(jnp.float32)
+    for member in range(1, slices):
+        expert_rows = expert_rows + partial_rows[member].astype(jnp.float32)
+    grad_hidden = jnp.dot(flat_grads, out_cat.T, preferred_element_type=jnp.float32)
     grad_pre = (grad_hidden * slope).astype(jnp.bfloat16)
     out_term = jnp.dot(hidden.T, flat_grads, preferred_element_type=jnp.float32)
     in_term = jnp.dot(flat_rows.T, grad_pre, preferred_element_type=jnp.float32)
-    grad_part = jnp.dot(grad_pre, in_weights.T, preferred_element_type=jnp.float32).astype(
-        jnp.bfloat16
-    )
-
+    grad_parts = jnp.einsum(
+        "rsh,sdh->srd", grad_pre.reshape(n_rows, slices, hid), in_all,
+        preferred_element_type=jnp.float32,
+    ).astype(jnp.bfloat16)
+    grad_rows = grad_parts[0].astype(jnp.float32)
+    for member in range(1, slices):
+        grad_rows = grad_rows + grad_parts[member].astype(jnp.float32)
+
+    in_term = jnp.transpose(in_term.reshape(width, slices, hid), (1, 0, 2))
+    in_term = in_term.reshape(2, 2, width, hid).astype(jnp.bfloat16)
+    out_term = out_term.reshape(2, 2, hid, width).astype(jnp.bfloat16)
+    in_mine = lax.psum_scatter(
+        lax.psum_scatter(in_term, "c", scatter_dimension=0, tiled=True), "xl", scatter_dimension=1, tiled=True
+    ).reshape(width, hid)
+    out_mine = lax.psum_scatter(
+        lax.psum_scatter(out_term, "c", scatter_dimension=0, tiled=True), "xl", scatter_dimension=1, tiled=True
+    ).reshape(hid, width)
     dp_pair = [(0, 1), (1, 0)]
-    in_mine, out_mine = in_term.astype(jnp.bfloat16), out_term.astype(jnp.bfloat16)
     in_other = lax.ppermute(in_mine, "dp", dp_pair)
     out_other = lax.ppermute(out_mine, "dp", dp_pair)
     dp_first = lax.axis_index("dp") == 0
@@ -156,9 +178,7 @@
     grad_in = in_a + in_b
     grad_out = out_a + out_b
 
-    back = jnp.concatenate([partial_rows, grad_part], axis=1).reshape(rows_shape)
-    back = lax.psum_scatter(back, "c", scatter_dimension=0, tiled=True)
-    back = lax.psum_scatter(back, "xl", scatter_dimension=1, tiled=True)
+    back = jnp.concatenate([expert_rows, grad_rows], axis=1).astype(jnp.bfloat16)
     back = back.reshape(expert_count, capacity, 2 * width)
     totals = lax.all_to_all(back, GRP, split_axis=0, concat_axis=0, tiled=True)
     totals = totals.reshape(expert_count * capacity, 2 * width)
@@ -185,8 +205,11 @@
     )
     kernel_term = kernel_terms(padded, upstream_total, length, row_count)
     small = jnp.concatenate([kernel_term, gain_term[None, :], router_term.T], axis=0)
-    for axis in ("c", "xl", "y", "z", "dp"):
-        small = lax.psum(small, axis)
+    for axis, size in (("c", 2), ("xl", 2), ("y", 4), ("z", 8), ("dp", 2)):
+        bit = 1
+        while bit < size:
+            small = small + lax.ppermute(small, axis, [(i, i ^ bit) for i in range(size)])
+            bit *= 2
     grad_kernel = small[:length]
     grad_gain = small[length]
     grad_router = small[length + 1 :].T

time: 621 us -> 388 us (0.62)
  the two profiles are of different devices: /device:TPU:1 before, /device:TPU:6 now
where the time goes in v2:
time: 388 us; the launch traced here: 382 us
  waiting for transfers between devices  230 us (59%)
  starting transfers between devices  40.2 us (10%)
  local copies, waits for them, and re-layouts  38 us (10%)
  matrix products  34.8 us (9%)
  other arithmetic  23.5 us (6%)
  between operations  16.1 us (4%)
    ppermute x8, waiting for transfers between devices, body(): lax.ppermute(small, axis, [(i, i ^ bit) for i in range(size)])  77.4 us
    all_to_all x1, waiting for transfers between devices, body(): totals = lax.all_to_all(back, GRP, split_axis=0, concat_axis=0, tiled=True)  39.9 us
    all_gather x1, waiting for transfers between devices, body(): lax.all_gather(in_weights, 'xl', axis=0)  36.8 us
    all_gather x1, waiting for transfers between devices, body(): lax.all_gather(out_weights, 'xl', axis=0)  22.3 us
    all_gather x1, waiting for transfers between devices, body(): lax.all_gather(lax.all_gather(in_weights, 'xl', axis=0), 'c', axis=0)  22.2 us
    ppermute x1, waiting for transfers between devices, body(): out_other = lax.ppermute(out_mine, 'dp', dp_pair)  17.9 us
    convert_element_type x2, local copies, waits for them, and re-layouts, body(): in_term = in_term.reshape(2, 2, width, hid).astype(jnp.bfloat16)  12.8 us
    all_to_all x1, starting transfers between devices, body(): lax.all_to_all(packed, GRP, split_axis=0, concat_axis=0, tiled=True)  9.85 us
  transfers between devices with their start and end apart: 24, of which 15 were waited for; matrix products, arithmetic and copies ran while one was open for 18% of the time, Pallas kernels for 0%

profile of v2, /device:TPU:6, one launch (start us, length us, event | category | flops | bytes accessed | tf_op | source)
XLA Modules:
  0.0 382.5 jit_solution(3825074724354741218)
XLA Ops:
  7.3 0.7 all-gather.7.cloned.1.call-update
  8.0 0.7 all-gather.9.cloned.1.call-update
  8.8 2.2 collective-permute-start.1
  11.0 2.2 collective-permute-start
  13.5 36.8 %all-gather.7.cloned.1.call-done = bf16[2,1024,512]{2,1,0:T(8,128)(2,1)} async-done(((bf16[1,1024,512]{2,1,0:T(8,128)(2,1)}), bf16[2,1024,512]{2,1,0:T(8,128)(2,1)}) %all-gather.7.cloned.1.call-update) | async-done | bytes 2097168 | tf_op jit(solution)/shard_map/all_gather | solution.py:126
  51.8 2.6 multiply_reduce_fusion.2
  57.0 2.0 convolution_convert_fusion.2
  59.1 9.9 %all-to-all-start = ((bf16[32,16,2048]{2,1,0:T(8,128)(2,1)}), bf16[32,16,2048]{2,1,0:T(8,128)(2,1)S(1)}, u32[]{:S(2)}, u32[]{:S(2)}) async-start(bf16[32,16,2048]{2,1,0:T(8,128)(2,1)} %bitcast.39), calls=%async_computation | async-start | bytes 4194304 | tf_op jit(solution)/shard_map/all_to_all | solution.py:125
  69.0 22.3 %all-gather.9.cloned.1.call-done = bf16[2,512,1024]{2,1,0:T(8,128)(2,1)} async-done(((bf16[1,512,1024]{2,1,0:T(8,128)(2,1)}), bf16[2,512,1024]{2,1,0:T(8,128)(2,1)}) %all-gather.9.cloned.1.call-update) | async-done | bytes 2097168 | tf_op jit(solution)/shard_map/all_gather | solution.py:127
  91.5 22.2 %all-gather.11.cloned.1.call-done = bf16[4,1024,512]{2,1,0:T(8,128)(2,1)} async-done(((bf16[2,1024,512]{2,1,0:T(8,128)(2,1)}), bf16[4,1024,512]{2,1,0:T(8,128)(2,1)}) %all-gather.11.cloned.1.call-update) | async-done | bytes 4194320 | tf_op jit(solution)/shard_map/all_gather | solution.py:126
  113.7 6.2 %copy.59 = bf16[4,1024,512]{1,2,0:T(8,128)(2,1)} copy(bf16[4,1024,512]{2,1,0:T(8,128)(2,1)} %all-gather.11.cloned.1.call-done) | data formatting | bytes 8388608 | tf_op jit(solution)/shard_map/all_gather | solution.py:126
  120.0 7.6 %multiply_convert_fusion.1 = (bf16[512,2048]{1,0:T(8,128)(2,1)}, f32[512,2048]{1,0:T(8,128)}) fusion(bf16[1024,2048]{0,1:T(8,128)(2,1)} %bitcast.193, bf16[512,2048]{1,0:T(8,128)(2,1)S(1)} %bitcast.196), kind=kOutput, calls=%fused_computation.2 | convolution fusion | flops 2152726528 | bytes 11534336 | tf_op jit(solution)/shard_map/dot_general | solution.py:139
  127.6 8.1 %all-gather.13.cloned.1.call-done = bf16[4,512,1024]{2,1,0:T(8,128)(2,1)} async-done(((bf16[2,512,1024]{2,1,0:T(8,128)(2,1)}), bf16[4,512,1024]{2,1,0:T(8,128)(2,1)}) %all-gather.13.cloned.1.call-update) | async-done | bytes 4194320 | tf_op jit(solution)/shard_map/all_gather | solution.py:127
  135.7 5.9 %multiply_convert_fusion = bf16[512,2048]{1,0:T(8,128)(2,1)S(1)} fusion(f32[512,2048]{1,0:T(8,128)} %get-tuple-element.89, bf16[2048,1024]{1,0:T(8,128)(2,1)} %bitcast.300, bf16[512,2048]{1,0:T(8,128)(2,1)S(1)} %bitcast.197), kind=kOutput, calls=%fused_computation.1 | convolution fusion | flops 2156920832 | bytes 11534336 | tf_op jit(solution)/shard_map/dot_general | solution.py:149
  141.6 1.3 copy-done.79
  142.9 4.4 %convolution_convert_fusion.1 = bf16[1024,2048]{1,0:T(8,128)(2,1)} fusion(bf16[512,2048]{1,0:T(8,128)(2,1)S(1)} %multiply_convert_fusion, bf16[512,2048]{1,0:T(8,128)(2,1)S(1)} %bitcast.198), kind=kOutput, calls=%fused_computation.5 | convolution fusion | flops 2149580800 | bytes 7340032 | tf_op jit(solution)/shard_map/dot_general | solution.py:152
  147.3 7.9 %convert_element_type.428 = bf16[1024,4,512]{2,1,0:T(4,128)(2,1)} reshape(bf16[1024,2048]{1,0:T(8,128)(2,1)} %convolution_convert_fusion.1) | data formatting | bytes 8388608 | tf_op jit(solution)/shard_map/convert_element_type | solution.py:162
  155.1 5.0 %copy.64 = bf16[4,1024,512]{2,1,0:T(8,128)(2,1)} copy(bf16[4,1024,512]{2,0,1:T(4,128)(2,1)} %bitcast.186) | data formatting | bytes 8388608 | tf_op jit(solution)/shard_map/convert_element_type | solution.py:162
  160.4 5.9 %convolution_convert_fusion = bf16[2048,1024]{1,0:T(8,128)(2,1)} fusion(bf16[512,2048]{1,0:T(8,128)(2,1)} %get-tuple-element.88, bf16[512,2048]{1,0:T(8,128)(2,1)S(1)} %bitcast.199), kind=kOutput, calls=%fused_computation.4 | convolution fusion | flops 2149580800 | bytes 7340032 | tf_op jit(solution)/shard_map/dot_general | solution.py:151
  166.4 5.3 %convolution_convert_fusion.3 = bf16[4,512,1024]{2,1,0:T(8,128)(2,1)S(1)} fusion(bf16[4,1024,512]{2,1,0:T(8,128)(2,1)} %all-gather.11.cloned.1.call-done, bf16[64,4,8,512]{3,2,1,0:T(8,128)(2,1)} %bitcast.302), kind=kOutput, calls=%fused_computation.7 | convolution fusion | flops 2149580800 | bytes 10485760 | tf_op jit(solution)/shard_map/rsh,sdh->srd/dot_general | solution.py:153
  171.7 0.9 add_convert_fusion
  172.6 2.0 copy-done.77
  174.6 2.3 convolution_convert_fusion.4
  177.0 0.9 add_convert_fusion.1
  177.9 1.5 pad_maximum_fusion
  179.4 9.8 %all-to-all-start.1 = ((bf16[32,16,2048]{2,1,0:T(8,128)(2,1)}), bf16[32,16,2048]{2,1,0:T(8,128)(2,1)S(1)}, u32[]{:S(2)}, u32[]{:S(2)}) async-start(bf16[32,16,2048]{2,1,0:T(8,128)(2,1)} %pad_maximum_fusion), calls=%async_computation.1 | async-start | bytes 4194304 | tf_op jit(solution)/shard_map/all_to_all | solution.py:183
  189.3 0.7 reduce-scatter.7.cloned.1.call-update
  190.3 1.4 reduce_sum.361
  191.7 1.2 broadcast_multiply_fusion
  193.0 1.4 copy.62
  194.4 1.5 mul.1012
  195.9 1.5 copy.57
  197.4 0.7 compare_select_fusion
  198.1 0.6 pad_clamp_fusion
  198.7 1.2 compare_and_fusion
  199.9 39.9 %all-to-all-done.1 = bf16[32,16,2048]{2,1,0:T(8,128)(2,1)S(1)} async-done(((bf16[32,16,2048]{2,1,0:T(8,128)(2,1)}), bf16[32,16,2048]{2,1,0:T(8,128)(2,1)S(1)}, u32[]{:S(2)}, u32[]{:S(2)}) %all-to-all-start.1) | async-done | bytes 2097184 | tf_op jit(solution)/shard_map/all_to_all | solution.py:183
  239.8 2.5 gather_fusion
  242.3 2.5 gather.7
  244.8 1.9 fusion.8
  246.8 1.6 fusion.82
  248.5 0.9 multiply_reduce_fusion
  249.6 0.9 fusion.78
  251.5 0.7 fusion.58
  252.6 1.5 collective-permute-done.4
  254.1 0.9 collective-permute-start.5
  255.1 13.4 %collective-permute-done.5 = f32[64,1024]{1,0:T(8,128)S(1)} collective-permute-done((f32[64,1024]{1,0:T(8,128)S(1)}, f32[64,1024]{1,0:T(8,128)S(1)}, u32[]{:S(2)}, u32[]{:S(2)}) %collective-permute-start.5) | collective-permute-done | bytes 262176 | tf_op jit(solution)/shard_map/ppermute | solution.py:211
  269.1 7.2 %collective-permute-done.6 = f32[64,1024]{1,0:T(8,128)S(1)} collective-permute-done((f32[64,1024]{1,0:T(8,128)S(1)}, f32[64,1024]{1,0:T(8,128)S(1)}, u32[]{:S(2)}, u32[]{:S(2)}) %collective-permute-start.6) | collective-permute-done | bytes 262176 | tf_op jit(solution)/shard_map/ppermute | solution.py:211
  276.6 1.1 collective-permute-start.7
  277.8 7.4 %collective-permute-done.7 = f32[64,1024]{1,0:T(8,128)S(1)} collective-permute-done((f32[64,1024]{1,0:T(8,128)S(1)}, f32[64,1024]{1,0:T(8,128)S(1)}, u32[]{:S(2)}, u32[]{:S(2)}) %collective-permute-start.7) | collective-permute-done | bytes 262176 | tf_op jit(solution)/shard_map/ppermute | solution.py:211
  285.3 6.4 %collective-permute-done.8 = f32[64,1024]{1,0:T(8,128)S(1)} collective-permute-done((f32[64,1024]{1,0:T(8,128)S(1)}, f32[64,1024]{1,0:T(8,128)S(1)}, u32[]{:S(2)}, u32[]{:S(2)}) %collective-permute-start.8) | collective-permute-done | bytes 262176 | tf_op jit(solution)/shard_map/ppermute | solution.py:211
  291.7 4.3 %collective-permute-start.9 = (f32[64,1024]{1,0:T(8,128)S(1)}, f32[64,1024]{1,0:T(8,128)S(1)}, u32[]{:S(2)}, u32[]{:S(2)}) collective-permute-start(f32[64,1024]{1,0:T(8,128)S(1)} %add.440), channel_id=1, source_target_pairs={{0,64},{32,96},{64,0},{96,32},{128,192},{160,224},{192,128},{224,1... | collective-permute-start | bytes 786440 | tf_op jit(solution)/shard_map/ppermute | solution.py:211
  296.0 18.0 %collective-permute-done.9 = f32[64,1024]{1,0:T(8,128)S(1)} collective-permute-done((f32[64,1024]{1,0:T(8,128)S(1)}, f32[64,1024]{1,0:T(8,128)S(1)}, u32[]{:S(2)}, u32[]{:S(2)}) %collective-permute-start.9) | collective-permute-done | bytes 262176 | tf_op jit(solution)/shard_map/ppermute | solution.py:211
  314.1 1.9 collective-permute-start.3
  316.1 2.4 collective-permute-start.2
  318.6 3.0 collective-permute-done.2
  321.7 2.7 collective-permute-done.10
  324.6 3.5 collective-permute-start.13
  328.3 2.8 fusion.147
  331.1 20.9 %collective-permute-done.11 = f32[64,1024]{1,0:T(8,128)S(1)} collective-permute-done((f32[64,1024]{1,0:T(8,128)S(1)}, f32[64,1024]{1,0:T(8,128)S(1)}, u32[]{:S(2)}, u32[]{:S(2)}) %collective-permute-start.11) | collective-permute-done | bytes 262176 | tf_op jit(solution)/shard_map/ppermute | solution.py:211
  352.0 0.7 slice.673
  353.2 0.7 slice_bitcast_fusion.2
  353.9 1.7 add_bitcast_fusion.1
  355.6 17.9 %collective-permute-done.13 = bf16[512,1024]{1,0:T(8,128)(2,1)S(1)} collective-permute-done((bf16[512,1024]{1,0:T(8,128)(2,1)}, bf16[512,1024]{1,0:T(8,128)(2,1)S(1)}, u32[]{:S(2)}, u32[]{:S(2)}) %collective-permute-start.13) | collective-permute-done | bytes 1048608 | tf_op jit(solution)/shard_map/ppermute | solution.py:172
  373.5 1.7 add_bitcast_fusion
  (227 shorter events, 8.6 us)
Async XLA Ops:
  7.2 48.1 %copy-start = (bf16[1024,32]{0,1:T(8,128)(2,1)S(1)}, bf16[1024,32]{0,1:T(8,128)(2,1)}, u32[]{:S(2)}) copy-start(bf16[1024,32]{0,1:T(8,128)(2,1)} %param.11) | copy-start | bytes 196612
  7.2 5.9 %copy-start.65 = (s32[1,128,2]{1,2,0:T(2,128)S(1)}, s32[1,128,2]{1,2,0:T(2,128)}, u32[]{:S(2)}) copy-start(s32[1,128,2]{1,2,0:T(2,128)} %param.12) | copy-start | bytes 3076
  7.2 44.1 %copy-start.5 = (bf16[31,1024]{1,0:T(8,128)(2,1)S(1)}, bf16[31,1024]{1,0:T(8,128)(2,1)}, u32[]{:S(2)}) copy-start(bf16[31,1024]{1,0:T(8,128)(2,1)} %param.9) | copy-start | bytes 190468
  7.2 43.1 %all-gather.7.cloned.1.call-start = ((), (), s32[]{:S(2)}) async-start(), calls=%async_computation.6 | async-start | bytes 3145728 | tf_op jit(solution)/shard_map/all_gather | solution.py:126
  7.9 83.3 %all-gather.9.cloned.1.call-start = ((), (), s32[]{:S(2)}) async-start(), calls=%async_computation.7 | async-start | bytes 3145728 | tf_op jit(solution)/shard_map/all_gather | solution.py:127
  8.7 46.1 %copy-start.6 = (f32[1024]{0:T(1024)S(1)}, f32[1024]{0:T(1024)}, u32[]{:S(2)}) copy-start(f32[1024]{0:T(1024)} %param.10) | copy-start | bytes 12292
  8.7 105.0 %all-gather.11.cloned.1.call-start = ((), (), s32[]{:S(2)}) async-start(), calls=%async_computation.12 | async-start | bytes 6291456 | tf_op jit(solution)/shard_map/all_gather | solution.py:126
  8.8 42.9 %collective-permute-start.1 = (bf16[15,1024]{1,0:T(8,128)(2,1)S(1)}, bf16[15,1024]{1,0:T(8,128)(2,1)S(1)}, u32[]{:S(2)}, u32[]{:S(2)}) collective-permute-start(bf16[15,1024]{1,0:T(8,128)(2,1)S(1)} %get-tuple-element.54), channel_id=1, source_target_pairs={{2,0},{4,2},{6,4},{8,6},{10,8},{12,10},{14,12},{16,14},{18,16},{20... | collective-permute-start | bytes 92168 | tf_op jit(solution)/shard_map/ppermute | solution.py:20
  11.0 40.8 %collective-permute-start = (bf16[15,1024]{1,0:T(8,128)(2,1)S(1)}, bf16[15,1024]{1,0:T(8,128)(2,1)S(1)}, u32[]{:S(2)}, u32[]{:S(2)}) collective-permute-start(bf16[15,1024]{1,0:T(8,128)(2,1)S(1)} %get-tuple-element.53), channel_id=1, source_target_pairs={{0,2},{2,4},{4,6},{6,8},{8,10},{10,12},{12,14},{14,16},{16,18},{18... | collective-permute-start | bytes 92168 | tf_op jit(solution)/shard_map/ppermute | solution.py:19
  50.3 5.2 %copy-start.2 = (bf16[1,128,1024]{2,1,0:T(8,128)(2,1)S(1)}, bf16[1,128,1024]{2,1,0:T(8,128)(2,1)}, u32[]{:S(2)}) copy-start(bf16[1,128,1024]{2,1,0:T(8,128)(2,1)} %param.15) | copy-start | bytes 786436
  51.3 3.1 copy-start.7
  51.4 3.1 copy-start.9
  51.7 4.6 %copy-start.66 = (s32[128]{0:T(128)}, s32[128]{0:T(128)S(1)}, u32[]{:S(2)}) copy-start(s32[128]{0:T(128)S(1)} %get-tuple-element.86) | copy-start | bytes 1540
  51.7 4.6 %copy-start.68 = (s32[128]{0:T(128)}, s32[128]{0:T(128)S(1)}, u32[]{:S(2)}) copy-start(s32[128]{0:T(128)S(1)} %get-tuple-element.87) | copy-start | bytes 1540
  59.1 60.9 %all-to-all-start = ((bf16[32,16,2048]{2,1,0:T(8,128)(2,1)}), bf16[32,16,2048]{2,1,0:T(8,128)(2,1)S(1)}, u32[]{:S(2)}, u32[]{:S(2)}) async-start(bf16[32,16,2048]{2,1,0:T(8,128)(2,1)} %bitcast.39), calls=%async_computation | async-start | bytes 4194304 | tf_op jit(solution)/shard_map/all_to_all | solution.py:125
  68.9 66.8 %all-gather.13.cloned.1.call-start = ((), (), s32[]{:S(2)}) async-start(), calls=%async_computation.13 | async-start | bytes 6291456 | tf_op jit(solution)/shard_map/all_gather | solution.py:127
  91.3 98.0 %reduce-scatter.5.cloned.1.call-start = ((), (), s32[]{:S(2)}) async-start(), calls=%async_computation.8 | async-start | bytes 6291456 | tf_op jit(solution)/shard_map/reduce_scatter | solution.py:165
  160.2 86.6 %reduce-scatter.9.cloned.1.call-start = ((), (), s32[]{:S(2)}) async-start(), calls=%async_computation.10 | async-start | bytes 6291456 | tf_op jit(solution)/shard_map/reduce_scatter | solution.py:168
  166.4 6.3 %copy-start.78 = (bf16[512,2048]{1,0:T(8,128)(2,1)S(1)}, bf16[512,2048]{1,0:T(8,128)(2,1)}, u32[]{:S(2)}) copy-start(bf16[512,2048]{1,0:T(8,128)(2,1)} %get-tuple-element.88) | copy-start | bytes 6291460
  179.4 60.5 %all-to-all-start.1 = ((bf16[32,16,2048]{2,1,0:T(8,128)(2,1)}), bf16[32,16,2048]{2,1,0:T(8,128)(2,1)S(1)}, u32[]{:S(2)}, u32[]{:S(2)}) async-start(bf16[32,16,2048]{2,1,0:T(8,128)(2,1)} %pad_maximum_fusion), calls=%async_computation.1 | async-start | bytes 4194304 | tf_op jit(solution)/shard_map/all_to_all | solution.py:183
  189.2 129.3 %reduce-scatter.7.cloned.1.call-start = ((), (), s32[]{:S(2)}) async-start(), calls=%async_computation.9 | async-start | bytes 3145728 | tf_op jit(solution)/shard_map/reduce_scatter | solution.py:164
  190.0 134.6 %reduce-scatter.11.cloned.1.call-start = ((), (), s32[]{:S(2)}) async-start(), calls=%async_computation.11 | async-start | bytes 3145728 | tf_op jit(solution)/shard_map/reduce_scatter | solution.py:167
  252.5 1.6 collective-permute-start.4
  254.1 14.4 %collective-permute-start.5 = (f32[64,1024]{1,0:T(8,128)S(1)}, f32[64,1024]{1,0:T(8,128)S(1)}, u32[]{:S(2)}, u32[]{:S(2)}) collective-permute-start(f32[64,1024]{1,0:T(8,128)S(1)} %add.436), channel_id=1, source_target_pairs={{0,4},{4,0},{1,5},{5,1},{2,6},{6,2},{3,7},{7,3},{8,12},{12,8},{9,1... | collective-permute-start | bytes 786440 | tf_op jit(solution)/shard_map/ppermute | solution.py:211
  268.5 7.8 %collective-permute-start.6 = (f32[64,1024]{1,0:T(8,128)S(1)}, f32[64,1024]{1,0:T(8,128)S(1)}, u32[]{:S(2)}, u32[]{:S(2)}) collective-permute-start(f32[64,1024]{1,0:T(8,128)S(1)} %add.437), channel_id=1, source_target_pairs={{0,8},{8,0},{16,24},{24,16},{1,9},{9,1},{17,25},{25,17},{2,10},{10... | collective-permute-start | bytes 786440 | tf_op jit(solution)/shard_map/ppermute | solution.py:211
  276.4 51.7 %copy-start.8 = (f32[1,1024]{1,0:T(1,128)S(1)}, f32[1,1024]{1,0:T(1,128)}, u32[]{:S(2)}) copy-start(f32[1,1024]{1,0:T(1,128)} %copy-done.7) | copy-start | bytes 12292
  276.4 51.7 %copy-start.10 = (f32[1,1024]{1,0:T(1,128)S(1)}, f32[1,1024]{1,0:T(1,128)}, u32[]{:S(2)}) copy-start(f32[1,1024]{1,0:T(1,128)} %copy-done.9) | copy-start | bytes 12292
  276.4 51.7 %copy-start.12 = (f32[1,1024]{1,0:T(1,128)S(1)}, f32[1,1024]{1,0:T(1,128)}, u32[]{:S(2)}) copy-start(f32[1,1024]{1,0:T(1,128)} %copy-done.11) | copy-start | bytes 12292
  276.4 51.7 %copy-start.14 = (f32[1,1024]{1,0:T(1,128)S(1)}, f32[1,1024]{1,0:T(1,128)}, u32[]{:S(2)}) copy-start(f32[1,1024]{1,0:T(1,128)} %copy-done.13) | copy-start | bytes 12292
  276.4 51.7 %copy-start.16 = (f32[1,1024]{1,0:T(1,128)S(1)}, f32[1,1024]{1,0:T(1,128)}, u32[]{:S(2)}) copy-start(f32[1,1024]{1,0:T(1,128)} %copy-done.15) | copy-start | bytes 12292
  276.4 51.7 %copy-start.18 = (f32[1,1024]{1,0:T(1,128)S(1)}, f32[1,1024]{1,0:T(1,128)}, u32[]{:S(2)}) copy-start(f32[1,1024]{1,0:T(1,128)} %copy-done.17) | copy-start | bytes 12292
  276.4 51.7 %copy-start.20 = (f32[1,1024]{1,0:T(1,128)S(1)}, f32[1,1024]{1,0:T(1,128)}, u32[]{:S(2)}) copy-start(f32[1,1024]{1,0:T(1,128)} %copy-done.19) | copy-start | bytes 12292
  276.4 51.7 %copy-start.22 = (f32[1,1024]{1,0:T(1,128)S(1)}, f32[1,1024]{1,0:T(1,128)}, u32[]{:S(2)}) copy-start(f32[1,1024]{1,0:T(1,128)} %copy-done.21) | copy-start | bytes 12292
  276.4 51.7 %copy-start.24 = (f32[1,1024]{1,0:T(1,128)S(1)}, f32[1,1024]{1,0:T(1,128)}, u32[]{:S(2)}) copy-start(f32[1,1024]{1,0:T(1,128)} %copy-done.23) | copy-start | bytes 12292
  276.4 51.7 %copy-start.26 = (f32[1,1024]{1,0:T(1,128)S(1)}, f32[1,1024]{1,0:T(1,128)}, u32[]{:S(2)}) copy-start(f32[1,1024]{1,0:T(1,128)} %copy-done.25) | copy-start | bytes 12292
  276.5 51.7 %copy-start.28 = (f32[1,1024]{1,0:T(1,128)S(1)}, f32[1,1024]{1,0:T(1,128)}, u32[]{:S(2)}) copy-start(f32[1,1024]{1,0:T(1,128)} %copy-done.27) | copy-start | bytes 12292
  276.5 51.7 %copy-start.30 = (f32[1,1024]{1,0:T(1,128)S(1)}, f32[1,1024]{1,0:T(1,128)}, u32[]{:S(2)}) copy-start(f32[1,1024]{1,0:T(1,128)} %copy-done.29) | copy-start | bytes 12292
  276.5 51.7 %copy-start.32 = (f32[1,1024]{1,0:T(1,128)S(1)}, f32[1,1024]{1,0:T(1,128)}, u32[]{:S(2)}) copy-start(f32[1,1024]{1,0:T(1,128)} %copy-done.31) | copy-start | bytes 12292
  276.5 51.7 %copy-start.34 = (f32[1,1024]{1,0:T(1,128)S(1)}, f32[1,1024]{1,0:T(1,128)}, u32[]{:S(2)}) copy-start(f32[1,1024]{1,0:T(1,128)} %copy-done.33) | copy-start | bytes 12292
  276.5 51.7 %copy-start.36 = (f32[1,1024]{1,0:T(1,128)S(1)}, f32[1,1024]{1,0:T(1,128)}, u32[]{:S(2)}) copy-start(f32[1,1024]{1,0:T(1,128)} %copy-done.35) | copy-start | bytes 12292
  276.5 51.7 %copy-start.38 = (f32[1,1024]{1,0:T(1,128)S(1)}, f32[1,1024]{1,0:T(1,128)}, u32[]{:S(2)}) copy-start(f32[1,1024]{1,0:T(1,128)} %copy-done.37) | copy-start | bytes 12292
  276.5 51.7 %copy-start.40 = (f32[1,1024]{1,0:T(1,128)S(1)}, f32[1,1024]{1,0:T(1,128)}, u32[]{:S(2)}) copy-start(f32[1,1024]{1,0:T(1,128)} %copy-done.39) | copy-start | bytes 12292
  276.5 51.7 %copy-start.42 = (f32[1,1024]{1,0:T(1,128)S(1)}, f32[1,1024]{1,0:T(1,128)}, u32[]{:S(2)}) copy-start(f32[1,1024]{1,0:T(1,128)} %copy-done.41) | copy-start | bytes 12292
  276.5 51.7 %copy-start.44 = (f32[1,1024]{1,0:T(1,128)S(1)}, f32[1,1024]{1,0:T(1,128)}, u32[]{:S(2)}) copy-start(f32[1,1024]{1,0:T(1,128)} %copy-done.43) | copy-start | bytes 12292
  276.5 51.7 %copy-start.46 = (f32[1,1024]{1,0:T(1,128)S(1)}, f32[1,1024]{1,0:T(1,128)}, u32[]{:S(2)}) copy-start(f32[1,1024]{1,0:T(1,128)} %copy-done.45) | copy-start | bytes 12292
  276.6 51.7 %copy-start.48 = (f32[1,1024]{1,0:T(1,128)S(1)}, f32[1,1024]{1,0:T(1,128)}, u32[]{:S(2)}) copy-start(f32[1,1024]{1,0:T(1,128)} %copy-done.47) | copy-start | bytes 12292
  276.6 51.7 %copy-start.50 = (f32[1,1024]{1,0:T(1,128)S(1)}, f32[1,1024]{1,0:T(1,128)}, u32[]{:S(2)}) copy-start(f32[1,1024]{1,0:T(1,128)} %copy-done.49) | copy-start | bytes 12292
  276.6 51.7 %copy-start.52 = (f32[1,1024]{1,0:T(1,128)S(1)}, f32[1,1024]{1,0:T(1,128)}, u32[]{:S(2)}) copy-start(f32[1,1024]{1,0:T(1,128)} %copy-done.51) | copy-start | bytes 12292
  276.6 51.7 %copy-start.54 = (f32[1,1024]{1,0:T(1,128)S(1)}, f32[1,1024]{1,0:T(1,128)}, u32[]{:S(2)}) copy-start(f32[1,1024]{1,0:T(1,128)} %copy-done.53) | copy-start | bytes 12292
  276.6 51.7 %copy-start.56 = (f32[1,1024]{1,0:T(1,128)S(1)}, f32[1,1024]{1,0:T(1,128)}, u32[]{:S(2)}) copy-start(f32[1,1024]{1,0:T(1,128)} %copy-done.55) | copy-start | bytes 12292
  276.6 51.7 %copy-start.58 = (f32[1,1024]{1,0:T(1,128)S(1)}, f32[1,1024]{1,0:T(1,128)}, u32[]{:S(2)}) copy-start(f32[1,1024]{1,0:T(1,128)} %copy-done.57) | copy-start | bytes 12292
  276.6 51.7 %copy-start.60 = (f32[1,1024]{1,0:T(1,128)S(1)}, f32[1,1024]{1,0:T(1,128)}, u32[]{:S(2)}) copy-start(f32[1,1024]{1,0:T(1,128)} %copy-done.59) | copy-start | bytes 12292
  276.6 51.7 %copy-start.62 = (f32[1,1024]{1,0:T(1,128)S(1)}, f32[1,1024]{1,0:T(1,128)}, u32[]{:S(2)}) copy-start(f32[1,1024]{1,0:T(1,128)} %copy-done.61) | copy-start | bytes 12292
  276.6 8.5 %collective-permute-start.7 = (f32[64,1024]{1,0:T(8,128)S(1)}, f32[64,1024]{1,0:T(8,128)S(1)}, u32[]{:S(2)}, u32[]{:S(2)}) collective-permute-start(f32[64,1024]{1,0:T(8,128)S(1)} %add.438), channel_id=1, source_target_pairs={{0,16},{8,24},{16,0},{24,8},{1,17},{9,25},{17,1},{25,9},{2,18},{10... | collective-permute-start | bytes 786440 | tf_op jit(solution)/shard_map/ppermute | solution.py:211
  285.2 6.5 %collective-permute-start.8 = (f32[64,1024]{1,0:T(8,128)S(1)}, f32[64,1024]{1,0:T(8,128)S(1)}, u32[]{:S(2)}, u32[]{:S(2)}) collective-permute-start(f32[64,1024]{1,0:T(8,128)S(1)} %add.439), channel_id=1, source_target_pairs={{0,32},{32,0},{64,96},{96,64},{128,160},{160,128},{192,224},{224,1... | collective-permute-start | bytes 786440 | tf_op jit(solution)/shard_map/ppermute | solution.py:211
  291.7 22.3 %collective-permute-start.9 = (f32[64,1024]{1,0:T(8,128)S(1)}, f32[64,1024]{1,0:T(8,128)S(1)}, u32[]{:S(2)}, u32[]{:S(2)}) collective-permute-start(f32[64,1024]{1,0:T(8,128)S(1)} %add.440), channel_id=1, source_target_pairs={{0,64},{32,96},{64,0},{96,32},{128,192},{160,224},{192,128},{224,1... | collective-permute-start | bytes 786440 | tf_op jit(solution)/shard_map/ppermute | solution.py:211
  314.0 10.4 %collective-permute-start.10 = (f32[64,1024]{1,0:T(8,128)S(1)}, f32[64,1024]{1,0:T(8,128)S(1)}, u32[]{:S(2)}, u32[]{:S(2)}) collective-permute-start(f32[64,1024]{1,0:T(8,128)S(1)} %add.441), channel_id=1, source_target_pairs={{0,128},{32,160},{64,192},{96,224},{128,0},{160,32},{192,64},{224,... | collective-permute-start | bytes 786440 | tf_op jit(solution)/shard_map/ppermute | solution.py:211
  314.1 4.5 %collective-permute-start.3 = (bf16[15,1024]{1,0:T(8,128)(2,1)S(1)}, bf16[15,1024]{1,0:T(8,128)(2,1)S(1)}, u32[]{:S(2)}, u32[]{:S(2)}) collective-permute-start(bf16[15,1024]{1,0:T(8,128)(2,1)S(1)} %get-tuple-element.50), channel_id=1, source_target_pairs={{2,0},{4,2},{6,4},{8,6},{10,8},{12,10},{14,12},{16,14},{18,16},{20... | collective-permute-start | bytes 92168 | tf_op jit(solution)/shard_map/ppermute | solution.py:20
  316.1 5.6 %collective-permute-start.2 = (bf16[15,1024]{1,0:T(8,128)(2,1)S(1)}, bf16[15,1024]{1,0:T(8,128)(2,1)S(1)}, u32[]{:S(2)}, u32[]{:S(2)}) collective-permute-start(bf16[15,1024]{1,0:T(8,128)(2,1)S(1)} %get-tuple-element.49), channel_id=1, source_target_pairs={{0,2},{2,4},{4,6},{6,8},{8,10},{10,12},{12,14},{14,16},{16,18},{18... | collective-permute-start | bytes 92168 | tf_op jit(solution)/shard_map/ppermute | solution.py:19
  318.5 35.4 %collective-permute-start.12 = (bf16[1024,512]{1,0:T(8,128)(2,1)}, bf16[1024,512]{1,0:T(8,128)(2,1)S(1)}, u32[]{:S(2)}, u32[]{:S(2)}) collective-permute-start(bf16[1024,512]{1,0:T(8,128)(2,1)} %bitcast.200), channel_id=1, source_target_pairs={{0,1},{1,0},{2,3},{3,2},{4,5},{5,4},{6,7},{7,6},{8,9},{9,8},{10,11... | collective-permute-start | bytes 3145736 | tf_op jit(solution)/shard_map/ppermute | solution.py:171
  324.4 27.5 %collective-permute-start.11 = (f32[64,1024]{1,0:T(8,128)S(1)}, f32[64,1024]{1,0:T(8,128)S(1)}, u32[]{:S(2)}, u32[]{:S(2)}) collective-permute-start(f32[64,1024]{1,0:T(8,128)S(1)} %add.442), channel_id=1, source_target_pairs={{0,1},{1,0},{2,3},{3,2},{4,5},{5,4},{6,7},{7,6},{8,9},{9,8},{10,11... | collective-permute-start | bytes 786440 | tf_op jit(solution)/shard_map/ppermute | solution.py:211
  324.6 29.3 %copy-start.3 = (bf16[1,1,1024,512]{3,2,1,0:T(8,128)(2,1)S(1)}, bf16[1,1,1024,512]{3,2,1,0:T(8,128)(2,1)}, u32[]{:S(2)}) copy-start(bf16[1,1,1024,512]{3,2,1,0:T(8,128)(2,1)} %reduce-scatter.7.cloned.1.call-done) | copy-start | bytes 3145732
  324.6 48.9 %collective-permute-start.13 = (bf16[512,1024]{1,0:T(8,128)(2,1)}, bf16[512,1024]{1,0:T(8,128)(2,1)S(1)}, u32[]{:S(2)}, u32[]{:S(2)}) collective-permute-start(bf16[512,1024]{1,0:T(8,128)(2,1)} %bitcast.201), channel_id=1, source_target_pairs={{0,1},{1,0},{2,3},{3,2},{4,5},{5,4},{6,7},{7,6},{8,9},{9,8},{10,11... | collective-permute-start | bytes 3145736 | tf_op jit(solution)/shard_map/ppermute | solution.py:172
  353.9 19.6 %copy-start.4 = (bf16[1,1,512,1024]{3,2,1,0:T(8,128)(2,1)S(1)}, bf16[1,1,512,1024]{3,2,1,0:T(8,128)(2,1)}, u32[]{:S(2)}) copy-start(bf16[1,1,512,1024]{3,2,1,0:T(8,128)(2,1)} %reduce-scatter.11.cloned.1.call-done) | copy-start | bytes 3145732
  (40 other events, 101.5 us)
Sparse Core Ops, SparseCore 0:
  9.8 40.4 all-gather.6
  52.1 39.1 all-gather.8
  93.1 20.6 all-gather.10
  115.4 20.2 all-gather.12
  160.3 18.7 reduce-scatter.4
  181.5 18.7 reduce-scatter.8
  202.8 37.6 reduce-scatter.6
  246.9 39.5 reduce-scatter.10
